TPU v7x, 1024 devices: a whole 4x8x16 slice. The times are simulated.
1024 devices in a mesh: dp: 4 (over x), expert: 32 (over z, core), tensor: 8 (over y).
Axes of the slice: x: 4, y: 8, z: 16, core: 2. Of those that a mesh axis runs over, the one named last changes fastest.
Arguments:
- tokens: bfloat16 [8192, 4096], P(('dp', 'expert'), 'tensor'), may hold values from -6 to 6
- expert_ids: int32 [8192, 8], P(('dp', 'expert')), may hold values from 0 to 63, all different within a row; in each aligned block of 64 rows (0 to 63, 64 to 127, ...) at most 9 rows name the same one
- combine_weight: float32 [8192, 8], P(('dp', 'expert')), may hold values from 0.05 to 0.4
- w_gate: bfloat16 [64, 4096, 1536], P('expert', None, 'tensor'), may hold values from -0.09375 to 0.09375
- w_up: bfloat16 [64, 4096, 1536], P('expert', None, 'tensor'), may hold values from -0.09375 to 0.09375
- w_down: bfloat16 [64, 1536, 4096], P('expert', 'tensor'), may hold values from -0.15625 to 0.15625
Outputs:
- mixed: bfloat16 [8192, 4096], P(('dp', 'expert'), 'tensor')
- expert_load: float32 [64], replicated
Inputs may be any that keep to these rules, and one draw needn't show every extreme that they name: `expert_ids`: each row names 8 different experts. In the rows of one token group no expert is named by more than 9 rows, and that most is reached.
All inputs are finite; a program needn't handle non-finite values.
Results may differ from a plain program's by a relative error of at most 0.015.
Values may be sent and summed in bfloat16 or wider, within the bound.
No kernel may reach another device: no remote copies, remote signals or barrier semaphores. Data moves between devices by JAX's collectives and lax.ppermute only.
A program may use at most 64 MiB of HBM per device.

v0:
```python
import jax
import jax.numpy as jnp
from jax import lax
from jax.sharding import PartitionSpec as P


def on_device(tokens, expert_ids, combine_weight, w_gate, w_up, w_down):
    owners = lax.axis_size("expert")
    splits = lax.axis_size("tensor")
    local = w_gate.shape[0]
    experts = owners * local
    tok_rows = tokens.shape[0]
    chosen = expert_ids.shape[1]
    capacity = min(tok_rows, (9 * tok_rows * chosen + 8 * experts - 1) // (8 * experts))
    flat_ids = expert_ids.reshape(-1)
    onehot = (flat_ids[:, None] == jnp.arange(experts, dtype=jnp.int32)[None, :]).astype(jnp.int32)
    ranks = jnp.sum((jnp.cumsum(onehot, axis=0) - onehot) * onehot, axis=1)
    target = flat_ids * capacity + ranks
    pair_count = flat_ids.shape[0]
    source = (
        jnp.full((experts * capacity,), -1, jnp.int32)
        .at[target]
        .set(jnp.arange(pair_count, dtype=jnp.int32) // chosen)
    )
    filled = (source >= 0)[:, None]
    safe = jnp.maximum(source, 0)
    outgoing = jnp.where(filled, tokens[safe], jnp.zeros((), jnp.bfloat16))
    outgoing = outgoing.reshape(owners, local * capacity, tokens.shape[1])
    sliced = lax.all_to_all(outgoing, "expert", split_axis=0, concat_axis=0, tiled=True)
    arrived = lax.all_gather(sliced, "tensor", axis=2, tiled=True)
    model_width = arrived.shape[2]
    stacked = arrived.reshape(owners, local, capacity, model_width)
    rows = jnp.transpose(stacked, (1, 0, 2, 3)).reshape(local, owners * capacity, model_width)
    gate = jnp.einsum("erd,edh->erh", rows, w_gate, preferred_element_type=jnp.float32)
    up = jnp.einsum("erd,edh->erh", rows, w_up, preferred_element_type=jnp.float32)
    hidden = (jax.nn.silu(gate) * up).astype(jnp.bfloat16)
    feature_cols = model_width // splits
    summed_out = lax.psum_scatter(
        jnp.einsum("erh,ehd->der", hidden, w_down, preferred_element_type=jnp.float32).astype(
            jnp.bfloat16
        ),
        "tensor",
        scatter_dimension=0,
        tiled=True,
    )
    expert_out = jnp.transpose(
        summed_out.reshape(feature_cols, local, owners, capacity), (2, 1, 3, 0)
    )
    expert_out = expert_out.reshape(owners, local * capacity, feature_cols)
    back = lax.all_to_all(expert_out, "expert", split_axis=0, concat_axis=0, tiled=True)
    back = back.reshape(experts * capacity, feature_cols)
    picked = back[target].astype(jnp.float32)
    weighted = picked * combine_weight.reshape(-1)[:, None]
    mixed = jnp.sum(weighted.reshape(tok_rows, chosen, feature_cols), axis=1).astype(jnp.bfloat16)
    group_load = jnp.sum(onehot.astype(jnp.float32) * combine_weight.reshape(-1)[:, None], axis=0)
    total_load = lax.psum(group_load, ("dp", "expert"))
    all_tokens = tok_rows * lax.axis_size("dp") * owners
    expert_load = total_load * (experts / all_tokens)
    return (mixed, expert_load)


def solution(mesh):
    in_specs = (
        P(("dp", "expert"), "tensor"),
        P(("dp", "expert"), None),
        P(("dp", "expert"), None),
        P("expert", None, "tensor"),
        P("expert", None, "tensor"),
        P("expert", "tensor", None),
    )
    out_specs = (P(("dp", "expert"), "tensor"), P())
    return jax.shard_map(
        on_device, mesh=mesh, in_specs=in_specs, out_specs=out_specs, check_vma=False
    )
```

profile of v0, /device:TPU:1, one launch (start us, length us, event | category | flops | bytes accessed | tf_op | source)
XLA Modules:
  0.0 568.6 jit_solution(8696360364787717735)
XLA Ops:
  7.2 0.0 copy-start
  7.2 0.0 all-gather.2.cloned.1.call-start
  7.2 0.9 copy.22
  8.1 0.1 eq.29
  8.2 0.1 eq.25
  8.3 0.7 broadcast_multiply_fusion
  9.0 1.2 reduce-window.6
  10.2 0.2 slice_reduce_fusion
  10.5 0.1 copy.21
  10.6 0.1 mul.53
  10.7 0.1 fusion.21
  10.8 2.4 scatter_custom_fusion
  13.3 4.1 gather_fusion
  17.5 2.1 gather.9
  19.5 0.1 broadcast_in_dim.25
  19.6 1.3 broadcast_select_fusion
  21.0 65.0 %all_to_all.10 = bf16[32,18,512]{2,1,0:T(8,128)(2,1)} all-to-all(bf16[32,18,512]{2,1,0:T(8,128)(2,1)S(1)} %broadcast_select_fusion), channel_id=1, replica_groups=mesh['dp'=4,'expert'=32,'tensor'=8] {'expert'}, dimensions={0} | all-to-all | bytes 1179648 | tf_op jit(solution)/shard_map/all_to_all | solution.py:29
  85.9 0.0 all-gather.2.cloned.1.call-update
  86.0 0.2 reduce-scatter.2.cloned.1.call-start
  86.2 73.1 %all-gather.2.cloned.1.call-done = bf16[32,18,4096]{2,1,0:T(8,128)(2,1)} async-done(((bf16[32,18,512]{2,1,0:T(8,128)(2,1)}), bf16[32,18,4096]{2,1,0:T(8,128)(2,1)}) %all-gather.2.cloned.1.call-update) | async-done | bytes 4718608 | tf_op jit(solution)/shard_map/all_gather | solution.py:30
  159.3 7.6 %copy.25 = bf16[32,18,4096]{2,0,1:T(8,128)(2,1)} copy(bf16[32,18,4096]{2,1,0:T(8,128)(2,1)} %all-gather.2.cloned.1.call-done) | data formatting | bytes 9437184 | tf_op jit(solution)/shard_map/all_gather | solution.py:30
  166.9 9.4 %copy.26 = bf16[2,32,9,4096]{3,0,2,1:T(2,128)(2,1)} copy(bf16[2,32,9,4096]{3,1,2,0:T(8,128)(2,1)} %bitcast.29) | data formatting | bytes 9437184 | tf_op jit(solution)/shard_map/transpose | solution.py:33
  176.3 7.1 %fusion.3 = f32[2,288,192]{2,1,0:T(8,128)} fusion(bf16[2,4096,192]{1,2,0:T(8,128)(2,1)} %param.9, bf16[2,288,4096]{2,0,1:T(2,128)(2,1)} %bitcast.30), kind=kOutput, calls=%fused_computation.7 | convolution fusion | flops 905969664 | bytes 8306688 | tf_op jit(solution)/shard_map/erd,edh->erh/dot_general | solution.py:34
  183.4 0.0 copy-done
  183.4 10.1 %fusion = bf16[4096,2,288]{0,2,1:T(8,128)(2,1)} fusion(bf16[2,192,4096]{2,1,0:T(8,128)(2,1)S(1)} %copy-done, bf16[2,4096,192]{1,2,0:T(8,128)(2,1)} %param.10, bf16[2,288,4096]{2,0,1:T(2,128)(2,1)} %bitcast.31, f32[2,288,192]{2,1,0:T(8,128)} %fusion.3), kind=kOutput, calls=%fused_computation.4 | convolution fusion | flops 1814962176 | bytes 16171008 | tf_op jit(solution)/shard_map/erh,ehd->der/dot_general | solution.py:39
  193.5 0.0 copy-start.1
  193.5 0.0 reduce-scatter.2.cloned.1.call-update
  193.5 67.4 %reduce-scatter.2.cloned.1.call-done = bf16[512,2,288]{0,2,1:T(8,128)(2,1)} async-done(((bf16[4096,2,288]{0,2,1:T(8,128)(2,1)}), bf16[512,2,288]{0,2,1:T(8,128)(2,1)}) %reduce-scatter.2.cloned.1.call-update) | async-done | bytes 589840 | tf_op jit(solution)/shard_map/reduce_scatter | solution.py:38
  260.9 1.7 copy.29
  262.6 0.1 copy.30
  262.7 1.2 copy.31
  263.9 13.7 %all-to-all-start.1 = ((bf16[32,18,512]{2,1,0:T(8,128)(2,1)}), bf16[32,18,512]{2,1,0:T(8,128)(2,1)}, u32[]{:S(2)}, u32[]{:S(2)}) async-start(bf16[32,18,512]{2,1,0:T(8,128)(2,1)} %copy.31), calls=%async_computation.2 | async-start | bytes 1572864 | tf_op jit(solution)/shard_map/all_to_all | solution.py:50
  277.7 0.0 copy-done.1
  277.7 0.1 copy.32
  277.8 0.1 mul.59
  277.9 0.1 fusion.23
  278.0 275.3 %psum.7 = f32[64]{0:T(128)S(1)} all-reduce(f32[64]{0:T(128)S(1)} %fusion.23), channel_id=1, replica_groups=mesh['dp'=4,'expert'=32,'tensor'=8] {'dp','expert'}, use_global_device_ids=true, to_apply=%region_7.8 | all-reduce | flops 64 | bytes 512 | tf_op jit(solution)/shard_map/psum | solution.py:56
  553.3 0.5 broadcast_multiply_fusion.1
  553.8 0.0 all-to-all-done.1
  553.8 2.1 reshape.88
  555.9 3.8 gather_fusion.1
  559.7 2.1 fusion.13
  (9 shorter events, 0.1 us)
Async XLA Ops:
  7.2 176.3 %copy-start = (bf16[2,192,4096]{2,1,0:T(8,128)(2,1)S(1)}, bf16[2,192,4096]{2,1,0:T(8,128)(2,1)}, u32[]{:S(2)}) copy-start(bf16[2,192,4096]{2,1,0:T(8,128)(2,1)} %param.11) | copy-start | bytes 9437188
  7.2 152.1 %all-gather.2.cloned.1.call-start = ((), (), s32[]{:S(2)}) async-start(), calls=%async_computation.3 | async-start | bytes 7077888 | tf_op jit(solution)/shard_map/all_gather | solution.py:30
  86.0 175.0 %reduce-scatter.2.cloned.1.call-start = ((), (), s32[]{:S(2)}) async-start(), calls=%async_computation.4 | async-start | bytes 5308416 | tf_op jit(solution)/shard_map/reduce_scatter | solution.py:38
  193.5 84.2 %copy-start.1 = (f32[64,8]{0,1:T(8,128)S(1)}, f32[64,8]{0,1:T(8,128)}, u32[]{:S(2)}) copy-start(f32[64,8]{0,1:T(8,128)} %param.8) | copy-start | bytes 6148
  263.9 289.9 %all-to-all-start.1 = ((bf16[32,18,512]{2,1,0:T(8,128)(2,1)}), bf16[32,18,512]{2,1,0:T(8,128)(2,1)}, u32[]{:S(2)}, u32[]{:S(2)}) async-start(bf16[32,18,512]{2,1,0:T(8,128)(2,1)} %copy.31), calls=%async_computation.2 | async-start | bytes 1572864 | tf_op jit(solution)/shard_map/all_to_all | solution.py:50
Sparse Core Ops, SparseCore 0:
  86.1 73.1 all-gather.1
  193.7 67.2 reduce-scatter.1
where the time goes:
time: 569 us
  blocking collectives  340 us (60%)
  waiting for transfers between devices  141 us (25%)
  local copies, waits for them, and re-layouts  36.3 us (6%)
  matrix products  17.2 us (3%)
  between operations  14.1 us (2%)
  starting transfers between devices  14 us (2%)
  other arithmetic  6.1 us (1%)
    psum x1, blocking collectives, on_device(): total_load = lax.psum(group_load, ('dp', 'expert'))  275 us
    all_gather x1, waiting for transfers between devices, on_device(): arrived = lax.all_gather(sliced, 'tensor', axis=2, tiled=True)  73.1 us
    reduce_scatter x1, waiting for transfers between devices, on_device(): lax.psum_scatter(jnp.einsum('erh,ehd->der', hidden, w_down, preferred_ele...  67.4 us
    all_to_all x1, blocking collectives, on_device(): lax.all_to_all(outgoing, 'expert', split_axis=0, concat_axis=0, tiled=True)  65 us
    all_to_all x1, starting transfers between devices, on_device(): lax.all_to_all(expert_out, 'expert', split_axis=0, concat_axis=0, tiled=T...  13.7 us
  transfers between devices with their start and end apart: 3, of which 2 were waited for; matrix products, arithmetic and copies ran while one was open for 0% of the time, Pallas kernels for 0%

commit v1 on v0

--- a/solution.py
+++ b/solution.py
@@ -53,7 +53,8 @@
     weighted = picked * combine_weight.reshape(-1)[:, None]
     mixed = jnp.sum(weighted.reshape(tok_rows, chosen, feature_cols), axis=1).astype(jnp.bfloat16)
     group_load = jnp.sum(onehot.astype(jnp.float32) * combine_weight.reshape(-1)[:, None], axis=0)
-    total_load = lax.psum(group_load, ("dp", "expert"))
+    row_load = jnp.sum(lax.all_gather(group_load, "expert", axis=0), axis=0)
+    total_load = jnp.sum(lax.all_gather(row_load, "dp", axis=0), axis=0)
     all_tokens = tok_rows * lax.axis_size("dp") * owners
     expert_load = total_load * (experts / all_tokens)
     return (mixed, expert_load)

time: 569 us -> 381 us (0.67)
  blocking collectives: 340 us -> 147 us
    psum x1 -> x0, blocking collectives: 275 us -> none  [on_device(): total_load = lax.psum(group_load, ('dp', 'expert'))]
    unnamed x0 -> x2, blocking collectives: none -> 82 us
  transfers between devices with their start and end apart: 3 -> 3, of which waited for: 2 -> 2; matrix products, arithmetic and copies ran while one was open for 0% -> 1% of each run, Pallas kernels for 0% -> 0%
where the time goes in v1:
time: 381 us; the launch traced here: 380 us
  blocking collectives  147 us (39%)
  waiting for transfers between devices  141 us (37%)
  local copies, waits for them, and re-layouts  39.5 us (10%)
  matrix products  17.2 us (5%)
  between operations  15.5 us (4%)
  starting transfers between devices  14 us (4%)
  other arithmetic  6.14 us (2%)
    unnamed x2, blocking collectives  82 us
    all_gather x1, waiting for transfers between devices, on_device(): arrived = lax.all_gather(sliced, 'tensor', axis=2, tiled=True)  73.1 us
    reduce_scatter x1, waiting for transfers between devices, on_device(): lax.psum_scatter(jnp.einsum('erh,ehd->der', hidden, w_down, preferred_ele...  67.4 us
    all_to_all x1, blocking collectives, on_device(): lax.all_to_all(outgoing, 'expert', split_axis=0, concat_axis=0, tiled=True)  65 us
    all_to_all x1, starting transfers between devices, on_device(): lax.all_to_all(expert_out, 'expert', split_axis=0, concat_axis=0, tiled=T...  13.7 us
    dot_general x1, matrix products, on_device(): jnp.einsum('erh,ehd->der', hidden, w_down, preferred_element_type=jnp.flo...  10.1 us
    transpose x1, local copies, waits for them, and re-layouts, on_device(): jnp.transpose(stacked, (1, 0, 2, 3))  9.41 us
  transfers between devices with their start and end apart: 3, of which 2 were waited for; matrix products, arithmetic and copies ran while one was open for 1% of the time, Pallas kernels for 0%

profile of v1, /device:TPU:1, one launch (start us, length us, event | category | flops | bytes accessed | tf_op | source)
XLA Modules:
  0.0 379.9 jit_solution(3744754243629623581)
XLA Ops:
  7.2 0.0 copy-start
  7.2 0.0 all-gather.4.cloned.1.call-start
  7.2 0.9 copy.35
  8.1 0.1 eq.29
  8.2 0.1 eq.25
  8.3 0.7 broadcast_multiply_fusion
  9.0 1.2 reduce-window.6
  10.2 0.2 slice_reduce_fusion
  10.5 0.1 copy.34
  10.6 0.1 mul.53
  10.7 0.1 fusion.21
  10.8 2.4 scatter_custom_fusion
  13.3 4.1 %gather_fusion = bf16[576,512]{1,0:T(8,128)(2,1)} fusion(bf16[64,512]{1,0:T(8,128)(2,1)} %param.6, s32[1024]{0:T(1024)S(1)} %pad_clamp_fusion.1), kind=kCustom, calls=%fused_computation | custom fusion | bytes 1181952 | tf_op jit(solution)/shard_map/gather | solution.py:27
  17.5 2.1 gather.9
  19.5 0.1 broadcast_in_dim.25
  19.6 1.3 broadcast_select_fusion
  21.0 65.0 %all_to_all.10 = bf16[32,18,512]{2,1,0:T(8,128)(2,1)} all-to-all(bf16[32,18,512]{2,1,0:T(8,128)(2,1)S(1)} %broadcast_select_fusion), channel_id=1, replica_groups=mesh['dp'=4,'expert'=32,'tensor'=8] {'expert'}, dimensions={0} | all-to-all | bytes 1179648 | tf_op jit(solution)/shard_map/all_to_all | solution.py:29
  85.9 0.0 all-gather.4.cloned.1.call-update
  86.0 0.2 reduce-scatter.2.cloned.1.call-start
  86.2 73.1 %all-gather.4.cloned.1.call-done = bf16[32,18,4096]{2,1,0:T(8,128)(2,1)} async-done(((bf16[32,18,512]{2,1,0:T(8,128)(2,1)}), bf16[32,18,4096]{2,1,0:T(8,128)(2,1)}) %all-gather.4.cloned.1.call-update) | async-done | bytes 4718608 | tf_op jit(solution)/shard_map/all_gather | solution.py:30
  159.3 7.6 %copy.38 = bf16[32,18,4096]{2,0,1:T(8,128)(2,1)} copy(bf16[32,18,4096]{2,1,0:T(8,128)(2,1)} %all-gather.4.cloned.1.call-done) | data formatting | bytes 9437184 | tf_op jit(solution)/shard_map/all_gather | solution.py:30
  166.9 9.4 %copy.39 = bf16[2,32,9,4096]{3,0,2,1:T(2,128)(2,1)} copy(bf16[2,32,9,4096]{3,1,2,0:T(8,128)(2,1)} %bitcast.31) | data formatting | bytes 9437184 | tf_op jit(solution)/shard_map/transpose | solution.py:33
  176.3 7.1 %fusion.3 = f32[2,288,192]{2,1,0:T(8,128)} fusion(bf16[2,4096,192]{1,2,0:T(8,128)(2,1)} %param.9, bf16[2,288,4096]{2,0,1:T(2,128)(2,1)} %bitcast.32), kind=kOutput, calls=%fused_computation.7 | convolution fusion | flops 905969664 | bytes 8306688 | tf_op jit(solution)/shard_map/erd,edh->erh/dot_general | solution.py:34
  183.4 0.0 copy-done
  183.4 10.1 %fusion = bf16[4096,2,288]{0,2,1:T(8,128)(2,1)} fusion(bf16[2,192,4096]{2,1,0:T(8,128)(2,1)S(1)} %copy-done, bf16[2,4096,192]{1,2,0:T(8,128)(2,1)} %param.10, bf16[2,288,4096]{2,0,1:T(2,128)(2,1)} %bitcast.33, f32[2,288,192]{2,1,0:T(8,128)} %fusion.3), kind=kOutput, calls=%fused_computation.4 | convolution fusion | flops 1814962176 | bytes 16171008 | tf_op jit(solution)/shard_map/erh,ehd->der/dot_general | solution.py:39
  193.5 0.0 reduce-scatter.2.cloned.1.call-update
  193.5 67.4 %reduce-scatter.2.cloned.1.call-done = bf16[512,2,288]{0,2,1:T(8,128)(2,1)} async-done(((bf16[4096,2,288]{0,2,1:T(8,128)(2,1)}), bf16[512,2,288]{0,2,1:T(8,128)(2,1)}) %reduce-scatter.2.cloned.1.call-update) | async-done | bytes 589840 | tf_op jit(solution)/shard_map/reduce_scatter | solution.py:38
  260.9 1.7 copy.42
  262.6 0.1 copy.43
  262.7 1.2 copy.44
  263.9 13.7 %all-to-all-start.1 = ((bf16[32,18,512]{2,1,0:T(8,128)(2,1)}), bf16[32,18,512]{2,1,0:T(8,128)(2,1)}, u32[]{:S(2)}, u32[]{:S(2)}) async-start(bf16[32,18,512]{2,1,0:T(8,128)(2,1)} %copy.44), calls=%async_computation.2 | async-start | bytes 1572864 | tf_op jit(solution)/shard_map/all_to_all | solution.py:50
  277.7 0.0 copy-done.1
  277.7 0.1 copy.45
  277.8 0.1 mul.59
  277.9 1.3 dynamic-slice
  279.8 0.1 fusion.23
  279.9 0.3 dynamic-update-slice
  280.2 73.6 %all-reduce = f32[2048]{0:T(1024)S(1)} all-reduce(f32[2048]{0:T(1024)S(1)} %dynamic-update-slice), channel_id=2, replica_groups=mesh['dp'=4,'expert'=32,'tensor'=8] {'expert'}, use_global_device_ids=true, to_apply=%add | all-reduce | flops 2048 | bytes 16384
  353.8 0.1 reshape.114
  353.9 1.3 dynamic-slice.1
  355.8 0.2 dynamic-update-slice.1
  356.1 8.4 %all-reduce.1 = f32[256]{0:T(256)S(1)} all-reduce(f32[256]{0:T(256)S(1)} %dynamic-update-slice.1), channel_id=3, replica_groups=mesh['dp'=4,'expert'=32,'tensor'=8] {'dp'}, use_global_device_ids=true, to_apply=%add.1 | all-reduce | flops 256 | bytes 2048
  364.5 0.1 reshape.115
  364.6 0.5 broadcast_multiply_fusion.1
  365.1 0.0 all-to-all-done.1
  365.1 2.1 reshape.88
  367.2 3.8 gather_fusion.1
  371.0 2.1 fusion.13
  (14 shorter events, 0.1 us)
Async XLA Ops:
  7.2 176.3 %copy-start = (bf16[2,192,4096]{2,1,0:T(8,128)(2,1)S(1)}, bf16[2,192,4096]{2,1,0:T(8,128)(2,1)}, u32[]{:S(2)}) copy-start(bf16[2,192,4096]{2,1,0:T(8,128)(2,1)} %param.11) | copy-start | bytes 9437188
  7.2 152.1 %all-gather.4.cloned.1.call-start = ((), (), s32[]{:S(2)}) async-start(), calls=%async_computation.3 | async-start | bytes 7077888 | tf_op jit(solution)/shard_map/all_gather | solution.py:30
  86.0 175.0 %reduce-scatter.2.cloned.1.call-start = ((), (), s32[]{:S(2)}) async-start(), calls=%async_computation.4 | async-start | bytes 5308416 | tf_op jit(solution)/shard_map/reduce_scatter | solution.py:38
  193.5 84.2 %copy-start.1 = (f32[64,8]{0,1:T(8,128)S(1)}, f32[64,8]{0,1:T(8,128)}, u32[]{:S(2)}) copy-start(f32[64,8]{0,1:T(8,128)} %param.8) | copy-start | bytes 6148
  263.9 101.2 %all-to-all-start.1 = ((bf16[32,18,512]{2,1,0:T(8,128)(2,1)}), bf16[32,18,512]{2,1,0:T(8,128)(2,1)}, u32[]{:S(2)}, u32[]{:S(2)}) async-start(bf16[32,18,512]{2,1,0:T(8,128)(2,1)} %copy.44), calls=%async_computation.2 | async-start | bytes 1572864 | tf_op jit(solution)/shard_map/all_to_all | solution.py:50
Sparse Core Ops, SparseCore 0:
  86.1 73.1 all-gather.3
  193.7 67.2 reduce-scatter.1

commit v2 on v0

v2 whole, which is shorter than its diff:
```python
import jax
import jax.numpy as jnp
from jax import lax
from jax.sharding import PartitionSpec as P


def on_device(tokens, expert_ids, combine_weight, w_gate, w_up, w_down):
    owners = lax.axis_size("expert")
    local = w_gate.shape[0]
    experts = owners * local
    tok_rows, feature_cols = tokens.shape
    chosen = expert_ids.shape[1]
    capacity = min(tok_rows, (9 * tok_rows * chosen + 8 * experts - 1) // (8 * experts))
    flat_ids = expert_ids.reshape(-1)
    onehot = (flat_ids[:, None] == jnp.arange(experts, dtype=jnp.int32)[None, :]).astype(jnp.int32)
    ranks = jnp.sum((jnp.cumsum(onehot, axis=0) - onehot) * onehot, axis=1)
    target = flat_ids * capacity + ranks
    pair_count = flat_ids.shape[0]
    source = (
        jnp.full((experts * capacity,), -1, jnp.int32)
        .at[target]
        .set(jnp.arange(pair_count, dtype=jnp.int32) // chosen)
    )
    filled = (source >= 0)[:, None]
    safe = jnp.maximum(source, 0)
    outgoing = jnp.where(filled, tokens[safe], jnp.zeros((), jnp.bfloat16))
    outgoing = outgoing.reshape(owners, local, capacity, feature_cols)
    group_load = jnp.sum(onehot.astype(jnp.float32) * combine_weight.reshape(-1)[:, None], axis=0)
    load_row = jnp.zeros((owners, 1, feature_cols), jnp.bfloat16)
    load_row = load_row.at[:, 0, :local].set(group_load.reshape(owners, local).astype(jnp.bfloat16))

    pieces = []
    owner_part = None
    total_load = None
    for c in range(local):
        send = outgoing[:, c]
        if c == 0:
            send = jnp.concatenate([send, load_row], axis=1)
        got = lax.all_to_all(send, "expert", split_axis=0, concat_axis=0, tiled=True)
        if c == 0:
            owner_part = jnp.sum(got[:, capacity, :local].astype(jnp.float32), axis=0)
            got = got[:, :capacity]
        arrived = lax.all_gather(got, "tensor", axis=2, tiled=True)
        model_width = arrived.shape[2]
        rows = arrived.reshape(owners * capacity, model_width)
        gate = jnp.dot(rows, w_gate[c], preferred_element_type=jnp.float32)
        up = jnp.dot(rows, w_up[c], preferred_element_type=jnp.float32)
        hidden = (jax.nn.silu(gate) * up).astype(jnp.bfloat16)
        down = jnp.einsum(
            "rh,hd->dr", hidden, w_down[c], preferred_element_type=jnp.float32
        ).astype(jnp.bfloat16)
        summed = lax.psum_scatter(down, "tensor", scatter_dimension=0, tiled=True)
        back_send = jnp.transpose(summed.reshape(feature_cols, owners, capacity), (1, 2, 0))
        if c == local - 1:
            owner_total = lax.psum(owner_part, "dp")
            total_row = jnp.zeros((owners, 1, feature_cols), jnp.bfloat16)
            total_row = total_row.at[:, 0, :local].set(
                jnp.broadcast_to(owner_total.astype(jnp.bfloat16)[None, :], (owners, local))
            )
            back_send = jnp.concatenate([back_send, total_row], axis=1)
        back = lax.all_to_all(back_send, "expert", split_axis=0, concat_axis=0, tiled=True)
        if c == local - 1:
            total_load = back[:, capacity, :local].astype(jnp.float32).reshape(experts)
            back = back[:, :capacity]
        pieces.append(back)
    back = jnp.stack(pieces, axis=1).reshape(experts * capacity, feature_cols)
    picked = back[target].astype(jnp.float32)
    weighted = picked * combine_weight.reshape(-1)[:, None]
    mixed = jnp.sum(weighted.reshape(tok_rows, chosen, feature_cols), axis=1).astype(jnp.bfloat16)
    all_tokens = tok_rows * lax.axis_size("dp") * owners
    expert_load = total_load * (experts / all_tokens)
    return (mixed, expert_load)


def solution(mesh):
    in_specs = (
        P(("dp", "expert"), "tensor"),
        P(("dp", "expert"), None),
        P(("dp", "expert"), None),
        P("expert", None, "tensor"),
        P("expert", None, "tensor"),
        P("expert", "tensor", None),
    )
    out_specs = (P(("dp", "expert"), "tensor"), P())
    return jax.shard_map(
        on_device, mesh=mesh, in_specs=in_specs, out_specs=out_specs, check_vma=False
    )
```

time: 569 us -> 356 us (0.63)
  blocking collectives: 340 us -> 99.6 us
  waiting for transfers between devices: 141 us -> 165 us
  starting transfers between devices: 14 us -> 34.8 us
  local copies, waits for them, and re-layouts: 36.3 us -> 20 us
    psum x1, blocking collectives: 275 us -> 8.41 us  [on_device(): owner_total = lax.psum(owner_part, 'dp')]
    all_to_all x1 -> x2, waiting for transfers between devices: 0.01 us -> 33.5 us  [on_device(): lax.all_to_all(back_send, 'expert', split_axis=0, concat_axis=0, tiled=True)]
    all_to_all x1 -> x2, blocking collectives: 65 us -> 91.2 us  [on_device(): lax.all_to_all(send, 'expert', split_axis=0, concat_axis=0, tiled=True)]
    all_to_all x1 -> x2, starting transfers between devices: 13.7 us -> 34.6 us  [on_device(): lax.all_to_all(back_send, 'expert', split_axis=0, concat_axis=0, tiled=True)]
    transpose x2 -> x0, local copies, waits for them, and re-layouts: 9.49 us -> none  [the longest x1 9.41 us: on_device(): jnp.transpose(stacked, (1, 0, 2, 3))]
    all_gather x1 -> x0, local copies, waits for them, and re-layouts: 7.58 us -> none  [on_device(): arrived = lax.all_gather(sliced, 'tensor', axis=2, tiled=True)]
    reshape x2 -> x5, local copies, waits for them, and re-layouts: 3.32 us -> 9.96 us  [the longest x2 6.74 us: on_device(): rows = arrived.reshape(owners * capacity, model_width)]
    all_gather x1 -> x2, waiting for transfers between devices: 73.1 us -> 68.4 us  [on_device(): arrived = lax.all_gather(got, 'tensor', axis=2, tiled=True)]
  transfers between devices with their start and end apart: 3 -> 6, of which waited for: 2 -> 5; matrix products, arithmetic and copies ran while one was open for 0% -> 8% of each run, Pallas kernels for 0% -> 0%
where the time goes in v2:
time: 356 us
  waiting for transfers between devices  165 us (46%)
  blocking collectives  99.6 us (28%)
  starting transfers between devices  34.8 us (10%)
  local copies, waits for them, and re-layouts  20 us (6%)
  matrix products  16.3 us (5%)
  between operations  14 us (4%)
  other arithmetic  5.57 us (2%)
    all_to_all x2, blocking collectives, on_device(): lax.all_to_all(send, 'expert', split_axis=0, concat_axis=0, tiled=True)  91.2 us
    all_gather x2, waiting for transfers between devices, on_device(): arrived = lax.all_gather(got, 'tensor', axis=2, tiled=True)  68.4 us
    reduce_scatter x2, waiting for transfers between devices, on_device(): summed = lax.psum_scatter(down, 'tensor', scatter_dimension=0, tiled=True)  63.4 us
    all_to_all x2, starting transfers between devices, on_device(): lax.all_to_all(back_send, 'expert', split_axis=0, concat_axis=0, tiled=True)  34.6 us
    all_to_all x2, waiting for transfers between devices, on_device(): lax.all_to_all(back_send, 'expert', split_axis=0, concat_axis=0, tiled=True)  33.5 us
    dot_general x2, matrix products, on_device(): jnp.einsum('rh,hd->dr', hidden, w_down[c], preferred_element_type=jnp.flo...  11.9 us
    psum x1, blocking collectives, on_device(): owner_total = lax.psum(owner_part, 'dp')  8.41 us
  transfers between devices with their start and end apart: 6, of which 5 were waited for; matrix products, arithmetic and copies ran while one was open for 8% of the time, Pallas kernels for 0%

profile of v2, /device:TPU:1, one launch (start us, length us, event | category | flops | bytes accessed | tf_op | source)
XLA Modules:
  0.0 355.6 jit_solution(14254109531937015493)
XLA Ops:
  7.2 0.8 copy.14
  8.0 0.1 eq.29
  8.1 0.1 eq.25
  8.2 0.7 broadcast_multiply_fusion
  8.9 1.2 reduce-window.6
  10.1 0.2 slice_reduce_fusion
  10.4 0.1 copy.13
  10.5 0.1 mul.62
  10.6 0.1 fusion.50
  10.7 2.4 scatter_custom_fusion
  13.2 2.7 gather_fusion
  15.9 0.2 gather.9
  16.2 0.2 broadcast_in_dim.29
  16.3 0.2 broadcast_select_fusion
  16.6 0.1 slice_bitcast_fusion.1
  16.7 53.8 %all_to_all.20 = bf16[32,9,512]{2,1,0:T(8,128)(2,1)} all-to-all(bf16[32,9,512]{2,1,0:T(8,128)(2,1)S(1)} %get-tuple-element.26), channel_id=1, replica_groups=mesh['dp'=4,'expert'=32,'tensor'=8] {'expert'}, dimensions={0} | all-to-all | bytes 589824 | tf_op jit(solution)/shard_map/all_to_all | solution.py:39
  70.5 0.0 all-gather.3.cloned.1.call-start
  70.6 0.1 copy.17
  70.7 0.1 mul.64
  70.8 0.1 fusion.52
  70.9 0.1 convert_element_type.79
  71.0 0.1 fusion.36
  71.1 37.4 %all_to_all.21 = bf16[32,10,512]{2,1,0:T(8,128)(2,1)} all-to-all(bf16[32,10,512]{2,1,0:T(8,128)(2,1)S(1)} %fusion.36), channel_id=1, replica_groups=mesh['dp'=4,'expert'=32,'tensor'=8] {'expert'}, dimensions={0} | all-to-all | bytes 655360 | tf_op jit(solution)/shard_map/all_to_all | solution.py:39
  108.5 15.6 %all-gather.5.cloned.1.call-done = bf16[32,9,4096]{2,1,0:T(8,128)(2,1)} async-done(((bf16[32,9,512]{2,1,0:T(8,128)(2,1)}), bf16[32,9,4096]{2,1,0:T(8,128)(2,1)}) %all-gather.5.cloned.1.call-update) | async-done | bytes 2359312 | tf_op jit(solution)/shard_map/all_gather | solution.py:43
  124.1 3.4 reshape.171
  127.5 2.2 fusion.5
  129.7 6.0 %fusion.1 = bf16[4096,288]{0,1:T(8,128)(2,1)} fusion(bf16[2,192,4096]{2,1,0:T(8,128)(2,1)} %param.15, bf16[288,4096]{1,0:T(8,128)(2,1)S(1)} %reshape.171, bf16[2,4096,192]{1,2,0:T(8,128)(2,1)} %param.14, f32[288,192]{1,0:T(8,128)S(1)} %fusion.5), kind=kOutput, calls=%fused_computation.6 | convolution fusion | flops 907481088 | bytes 8085504 | tf_op jit(solution)/shard_map/rh,hd->dr/dot_general | solution.py:49
  135.7 52.8 %all-gather.3.cloned.1.call-done = bf16[32,9,4096]{2,1,0:T(8,128)(2,1)} async-done(((bf16[32,9,512]{2,1,0:T(8,128)(2,1)}), bf16[32,9,4096]{2,1,0:T(8,128)(2,1)}) %all-gather.3.cloned.1.call-update) | async-done | bytes 2359312 | tf_op jit(solution)/shard_map/all_gather | solution.py:43
  188.5 3.4 reshape.169
  191.9 2.2 fusion.10
  194.1 6.0 %fusion = bf16[4096,288]{0,1:T(8,128)(2,1)} fusion(bf16[2,192,4096]{2,1,0:T(8,128)(2,1)} %param.15, bf16[288,4096]{1,0:T(8,128)(2,1)S(1)} %reshape.169, bf16[2,4096,192]{1,2,0:T(8,128)(2,1)} %param.14, f32[288,192]{1,0:T(8,128)S(1)} %fusion.10), kind=kOutput, calls=%fused_computation.5 | convolution fusion | flops 907481088 | bytes 8085504 | tf_op jit(solution)/shard_map/rh,hd->dr/dot_general | solution.py:49
  200.1 0.9 fusion.56
  201.0 8.4 %psum.7 = bf16[2]{0:T(256)(128)(2,1)S(1)} all-reduce(f32[2]{0:T(128)S(1)} %fusion.56), channel_id=1, replica_groups=mesh['dp'=4,'expert'=32,'tensor'=8] {'dp'}, use_global_device_ids=true, to_apply=%region_8.9 | all-reduce | flops 2 | bytes 12 | tf_op jit(solution)/shard_map/psum | solution.py:55
  209.4 28.8 %reduce-scatter.5.cloned.1.call-done = bf16[512,288]{0,1:T(8,128)(2,1)} async-done(((bf16[4096,288]{0,1:T(8,128)(2,1)}), bf16[512,288]{0,1:T(8,128)(2,1)}) %reduce-scatter.5.cloned.1.call-update) | async-done | bytes 294928 | tf_op jit(solution)/shard_map/reduce_scatter | solution.py:52
  238.2 1.1 reshape.172
  239.4 0.9 pad_maximum_fusion.1
  240.3 17.5 %all-to-all-start.3 = ((bf16[32,10,512]{2,1,0:T(8,128)(2,1)}), bf16[32,10,512]{2,1,0:T(8,128)(2,1)S(1)}, u32[]{:S(2)}, u32[]{:S(2)}) async-start(bf16[32,10,512]{2,1,0:T(8,128)(2,1)} %pad_maximum_fusion.1), calls=%async_computation.5 | async-start | bytes 1048576 | tf_op jit(solution)/shard_map/all_to_all | solution.py:61
  257.8 34.6 %reduce-scatter.3.cloned.1.call-done = bf16[512,288]{0,1:T(8,128)(2,1)} async-done(((bf16[4096,288]{0,1:T(8,128)(2,1)}), bf16[512,288]{0,1:T(8,128)(2,1)}) %reduce-scatter.3.cloned.1.call-update) | async-done | bytes 294928 | tf_op jit(solution)/shard_map/reduce_scatter | solution.py:52
  292.4 1.9 reshape.170
  294.3 17.1 %all-to-all-start.1 = ((bf16[32,9,512]{2,1,0:T(8,128)(2,1)}), bf16[32,9,512]{2,1,0:T(8,128)(2,1)S(1)}, u32[]{:S(2)}, u32[]{:S(2)}) async-start(bf16[32,9,512]{2,1,0:T(8,128)(2,1)} %bitcast.8), calls=%async_computation.2 | async-start | bytes 1048576 | tf_op jit(solution)/shard_map/all_to_all | solution.py:61
  311.5 33.5 %all-to-all-done.1 = bf16[32,9,512]{2,1,0:T(8,128)(2,1)S(1)} async-done(((bf16[32,9,512]{2,1,0:T(8,128)(2,1)}), bf16[32,9,512]{2,1,0:T(8,128)(2,1)S(1)}, u32[]{:S(2)}, u32[]{:S(2)}) %all-to-all-start.1) | async-done | bytes 294944 | tf_op jit(solution)/shard_map/all_to_all | solution.py:61
  344.9 0.1 pad_maximum_fusion
  345.1 0.1 copy.19
  345.2 0.3 reshape.173
  345.4 2.0 gather_fusion.1
  347.4 1.0 fusion.34
  348.4 0.1 fusion.55
  348.5 0.6 mul.75
  (24 shorter events, 0.4 us)
Async XLA Ops:
  7.2 6.0 %copy-start = (bf16[64,512]{1,0:T(8,128)(2,1)S(1)}, bf16[64,512]{1,0:T(8,128)(2,1)}, u32[]{:S(2)}) copy-start(bf16[64,512]{1,0:T(8,128)(2,1)} %param.10) | copy-start | bytes 196612
  7.2 116.9 %all-gather.5.cloned.1.call-start = ((), (), s32[]{:S(2)}) async-start(), calls=%async_computation.8 | async-start | bytes 4718592 | tf_op jit(solution)/shard_map/all_gather | solution.py:43
  16.6 54.0 %copy-start.1 = (f32[64,8]{0,1:T(8,128)S(1)}, f32[64,8]{0,1:T(8,128)}, u32[]{:S(2)}) copy-start(f32[64,8]{0,1:T(8,128)} %param.12) | copy-start | bytes 6148
  70.5 118.0 %all-gather.3.cloned.1.call-start = ((), (), s32[]{:S(2)}) async-start(), calls=%async_computation.6 | async-start | bytes 4718592 | tf_op jit(solution)/shard_map/all_gather | solution.py:43
  108.5 129.8 %reduce-scatter.5.cloned.1.call-start = ((), (), s32[]{:S(2)}) async-start(), calls=%async_computation.9 | async-start | bytes 2654208 | tf_op jit(solution)/shard_map/reduce_scatter | solution.py:52
  135.7 156.7 %reduce-scatter.3.cloned.1.call-start = ((), (), s32[]{:S(2)}) async-start(), calls=%async_computation.7 | async-start | bytes 2654208 | tf_op jit(solution)/shard_map/reduce_scatter | solution.py:52
  240.3 54.0 %all-to-all-start.3 = ((bf16[32,10,512]{2,1,0:T(8,128)(2,1)}), bf16[32,10,512]{2,1,0:T(8,128)(2,1)S(1)}, u32[]{:S(2)}, u32[]{:S(2)}) async-start(bf16[32,10,512]{2,1,0:T(8,128)(2,1)} %pad_maximum_fusion.1), calls=%async_computation.5 | async-start | bytes 1048576 | tf_op jit(solution)/shard_map/all_to_all | solution.py:61
  294.3 50.7 %all-to-all-start.1 = ((bf16[32,9,512]{2,1,0:T(8,128)(2,1)}), bf16[32,9,512]{2,1,0:T(8,128)(2,1)S(1)}, u32[]{:S(2)}, u32[]{:S(2)}) async-start(bf16[32,9,512]{2,1,0:T(8,128)(2,1)} %bitcast.8), calls=%async_computation.2 | async-start | bytes 1048576 | tf_op jit(solution)/shard_map/all_to_all | solution.py:61
Sparse Core Ops, SparseCore 0:
  70.6 53.4 all-gather.4
  126.8 61.7 all-gather.2
  192.0 46.2 reduce-scatter.4
  241.5 50.8 reduce-scatter.2

commit v3 on v0

v3 whole, which is shorter than its diff:
```python
import jax
import jax.numpy as jnp
from jax import lax
from jax.sharding import PartitionSpec as P


def on_device(tokens, expert_ids, combine_weight, w_gate, w_up, w_down):
    owners = lax.axis_size("expert")
    local = w_gate.shape[0]
    experts = owners * local
    tok_rows, feature_cols = tokens.shape
    chosen = expert_ids.shape[1]
    capacity = min(tok_rows, (9 * tok_rows * chosen + 8 * experts - 1) // (8 * experts))
    flat_ids = expert_ids.reshape(-1)
    onehot = (flat_ids[:, None] == jnp.arange(experts, dtype=jnp.int32)[None, :]).astype(jnp.int32)
    ranks = jnp.sum((jnp.cumsum(onehot, axis=0) - onehot) * onehot, axis=1)
    target = flat_ids * capacity + ranks
    pair_count = flat_ids.shape[0]
    source = (
        jnp.full((experts * capacity,), -1, jnp.int32)
        .at[target]
        .set(jnp.arange(pair_count, dtype=jnp.int32) // chosen)
    )
    filled = (source >= 0)[:, None]
    safe = jnp.maximum(source, 0)
    outgoing = jnp.where(filled, tokens[safe], jnp.zeros((), jnp.bfloat16))
    outgoing = outgoing.reshape(owners, local, capacity, feature_cols)
    group_load = jnp.sum(onehot.astype(jnp.float32) * combine_weight.reshape(-1)[:, None], axis=0)
    load_row = jnp.zeros((owners, 1, feature_cols), jnp.bfloat16)
    load_row = load_row.at[:, 0, :local].set(group_load.reshape(owners, local).astype(jnp.bfloat16))

    send = jnp.concatenate(
        [outgoing.reshape(owners, local * capacity, feature_cols), load_row], axis=1
    )
    got = lax.all_to_all(send, "expert", split_axis=0, concat_axis=0, tiled=True)
    owner_part = jnp.sum(got[:, local * capacity, :local].astype(jnp.float32), axis=0)
    got = got[:, : local * capacity].reshape(owners, local, capacity, feature_cols)
    got = jnp.transpose(got, (1, 0, 2, 3)).reshape(local * owners * capacity, feature_cols)
    arrived = lax.all_gather(got, "tensor", axis=1, tiled=True)
    model_width = arrived.shape[1]
    rows = arrived.reshape(local, owners * capacity, model_width)
    gate = jnp.einsum("erd,edh->erh", rows, w_gate, preferred_element_type=jnp.float32)
    up = jnp.einsum("erd,edh->erh", rows, w_up, preferred_element_type=jnp.float32)
    hidden = (jax.nn.silu(gate) * up).astype(jnp.bfloat16)
    down = jnp.einsum("erh,ehd->der", hidden, w_down, preferred_element_type=jnp.float32).astype(
        jnp.bfloat16
    )
    summed = lax.psum_scatter(down, "tensor", scatter_dimension=0, tiled=True)
    back_send = jnp.transpose(
        summed.reshape(feature_cols, local, owners, capacity), (2, 1, 3, 0)
    ).reshape(owners, local * capacity, feature_cols)
    owner_total = lax.psum(owner_part, "dp")
    total_row = jnp.zeros((owners, 1, feature_cols), jnp.bfloat16)
    total_row = total_row.at[:, 0, :local].set(
        jnp.broadcast_to(owner_total.astype(jnp.bfloat16)[None, :], (owners, local))
    )
    back_send = jnp.concatenate([back_send, total_row], axis=1)
    back = lax.all_to_all(back_send, "expert", split_axis=0, concat_axis=0, tiled=True)
    total_load = back[:, local * capacity, :local].astype(jnp.float32).reshape(experts)
    back = back[:, : local * capacity].reshape(experts * capacity, feature_cols)
    picked = back[target].astype(jnp.float32)
    weighted = picked * combine_weight.reshape(-1)[:, None]
    mixed = jnp.sum(weighted.reshape(tok_rows, chosen, feature_cols), axis=1).astype(jnp.bfloat16)
    all_tokens = tok_rows * lax.axis_size("dp") * owners
    expert_load = total_load * (experts / all_tokens)
    return (mixed, expert_load)


def solution(mesh):
    in_specs = (
        P(("dp", "expert"), "tensor"),
        P(("dp", "expert"), None),
        P(("dp", "expert"), None),
        P("expert", None, "tensor"),
        P("expert", None, "tensor"),
        P("expert", "tensor", None),
    )
    out_specs = (P(("dp", "expert"), "tensor"), P())
    return jax.shard_map(
        on_device, mesh=mesh, in_specs=in_specs, out_specs=out_specs, check_vma=False
    )
```

time: 569 us -> 309 us (0.54)
  blocking collectives: 340 us -> 73.3 us
  waiting for transfers between devices: 141 us -> 161 us
  local copies, waits for them, and re-layouts: 36.3 us -> 24.5 us
    psum x1, blocking collectives: 275 us -> 8.41 us  [on_device(): owner_total = lax.psum(owner_part, 'dp')]
    all_to_all x1, waiting for transfers between devices: 0.01 us -> 44.7 us  [on_device(): lax.all_to_all(back_send, 'expert', split_axis=0, concat_axis=0, tiled=True)]
    all_gather x1, waiting for transfers between devices: 73.1 us -> 58.6 us  [on_device(): arrived = lax.all_gather(got, 'tensor', axis=1, tiled=True)]
    reduce_scatter x1, waiting for transfers between devices: 67.4 us -> 58 us  [on_device(): summed = lax.psum_scatter(down, 'tensor', scatter_dimension=0, tiled=True)]
    transpose x2, local copies, waits for them, and re-layouts: 9.49 us -> 1.44 us  [the longest x1 1.37 us: on_device(): jnp.transpose(got, (1, 0, 2, 3))]
    all_gather x1 -> x0, local copies, waits for them, and re-layouts: 7.58 us -> none  [on_device(): arrived = lax.all_gather(sliced, 'tensor', axis=2, tiled=True)]
  transfers between devices with their start and end apart: 3 -> 3, of which waited for: 2 -> 3; matrix products, arithmetic and copies ran while one was open for 0% -> 0% of each run, Pallas kernels for 0% -> 0%
where the time goes in v3:
time: 309 us; the launch traced here: 308 us
  waiting for transfers between devices  161 us (52%)
  blocking collectives  73.3 us (24%)
  local copies, waits for them, and re-layouts  24.5 us (8%)
  between operations  14.2 us (5%)
  starting transfers between devices  13.8 us (4%)
  matrix products  13.8 us (4%)
  other arithmetic  7.57 us (2%)
    all_to_all x1, blocking collectives, on_device(): lax.all_to_all(send, 'expert', split_axis=0, concat_axis=0, tiled=True)  64.9 us
    all_gather x1, waiting for transfers between devices, on_device(): arrived = lax.all_gather(got, 'tensor', axis=1, tiled=True)  58.6 us
    reduce_scatter x1, waiting for transfers between devices, on_device(): summed = lax.psum_scatter(down, 'tensor', scatter_dimension=0, tiled=True)  58 us
    all_to_all x1, waiting for transfers between devices, on_device(): lax.all_to_all(back_send, 'expert', split_axis=0, concat_axis=0, tiled=True)  44.7 us
    all_to_all x1, starting transfers between devices, on_device(): lax.all_to_all(back_send, 'expert', split_axis=0, concat_axis=0, tiled=True)  13.8 us
    psum x1, blocking collectives, on_device(): owner_total = lax.psum(owner_part, 'dp')  8.41 us
    dot_general x1, matrix products, on_device(): jnp.einsum('erh,ehd->der', hidden, w_down, preferred_element_type=jnp.flo...  8.21 us
  transfers between devices with their start and end apart: 3, of which 3 were waited for; matrix products, arithmetic and copies ran while one was open for 0% of the time, Pallas kernels for 0%

profile of v3, /device:TPU:1, one launch (start us, length us, event | category | flops | bytes accessed | tf_op | source)
XLA Modules:
  0.0 308.5 jit_solution(824745130749700649)
XLA Ops:
  7.2 0.0 copy-start
  7.2 0.0 copy-start.1
  7.2 0.0 all-gather.2.cloned.1.call-start
  7.2 0.9 copy.37
  8.2 0.7 broadcast_multiply_fusion
  8.9 0.1 eq.25
  9.0 0.1 eq.29
  9.1 0.1 copy.36
  9.2 0.1 mul.56
  9.3 1.2 reduce-window.6
  10.5 0.2 slice_reduce_fusion
  10.7 0.1 fusion.12
  10.9 2.4 scatter_custom_fusion
  13.4 0.8 copy.40
  14.1 0.1 mul.58
  14.2 0.1 fusion.14
  14.3 0.1 convert_element_type.67
  14.5 0.0 copy-done.1
  14.5 3.2 %gather_fusion = bf16[576,512]{1,0:T(8,128)(2,1)} fusion(bf16[64,512]{1,0:T(8,128)(2,1)S(1)} %copy-done.1, s32[1024]{0:T(1024)S(1)} %pad_clamp_fusion.1), kind=kCustom, calls=%fused_computation | custom fusion | bytes 1181952 | tf_op jit(solution)/shard_map/gather | solution.py:26
  17.7 2.1 gather.9
  19.8 0.1 broadcast_in_dim.29
  19.9 1.3 broadcast_select_fusion
  21.2 0.1 fusion.4
  21.3 64.9 %all_to_all.10 = bf16[32,19,512]{2,1,0:T(8,128)(2,1)S(1)} all-to-all(bf16[32,19,512]{2,1,0:T(8,128)(2,1)S(1)} %fusion.4), channel_id=1, replica_groups=mesh['dp'=4,'expert'=32,'tensor'=8] {'expert'}, dimensions={0} | all-to-all | bytes 1245184 | tf_op jit(solution)/shard_map/all_to_all | solution.py:35
  86.2 0.9 copy-done.2
  87.1 0.2 copy.42
  87.3 1.4 copy.43
  88.7 2.2 reshape.172
  90.8 0.0 all-gather.2.cloned.1.call-update
  90.8 0.0 reduce-scatter.2.cloned.1.call-start
  90.9 58.6 %all-gather.2.cloned.1.call-done = bf16[576,4096]{1,0:T(8,128)(2,1)} async-done(((bf16[576,512]{1,0:T(8,128)(2,1)}), bf16[576,4096]{1,0:T(8,128)(2,1)}) %all-gather.2.cloned.1.call-update) | async-done | bytes 4718608 | tf_op jit(solution)/shard_map/all_gather | solution.py:39
  149.5 5.6 %fusion.25 = f32[2,288,192]{2,1,0:T(8,128)} fusion(bf16[2,288,4096]{2,1,0:T(8,128)(2,1)} %bitcast.40, bf16[2,4096,192]{1,2,0:T(8,128)(2,1)} %param.13), kind=kOutput, calls=%fused_computation.53 | convolution fusion | flops 905969664 | bytes 8306688 | tf_op jit(solution)/shard_map/erd,edh->erh/dot_general | solution.py:42
  155.1 8.2 %fusion = bf16[4096,2,288]{0,2,1:T(8,128)(2,1)} fusion(bf16[2,192,4096]{2,1,0:T(8,128)(2,1)S(1)} %copy-done, bf16[2,288,4096]{2,1,0:T(8,128)(2,1)} %bitcast.41, bf16[2,4096,192]{1,2,0:T(8,128)(2,1)} %param.14, f32[2,288,192]{2,1,0:T(8,128)} %fusion.25), kind=kOutput, calls=%fused_computation.4 | convolution fusion | flops 1814962176 | bytes 16171008 | tf_op jit(solution)/shard_map/erh,ehd->der/dot_general | solution.py:45
  163.3 0.0 reduce-scatter.2.cloned.1.call-update
  163.3 0.9 fusion.18
  164.2 8.4 %psum.7 = bf16[2]{0:T(256)(128)(2,1)S(1)} all-reduce(f32[2]{0:T(128)S(1)} %fusion.18), channel_id=1, replica_groups=mesh['dp'=4,'expert'=32,'tensor'=8] {'dp'}, use_global_device_ids=true, to_apply=%region_7.8 | all-reduce | flops 2 | bytes 12 | tf_op jit(solution)/shard_map/psum | solution.py:52
  172.6 58.0 %reduce-scatter.2.cloned.1.call-done = bf16[512,2,288]{0,2,1:T(8,128)(2,1)} async-done(((bf16[4096,2,288]{0,2,1:T(8,128)(2,1)}), bf16[512,2,288]{0,2,1:T(8,128)(2,1)}) %reduce-scatter.2.cloned.1.call-update) | async-done | bytes 589840 | tf_op jit(solution)/shard_map/reduce_scatter | solution.py:48
  230.6 1.7 copy.44
  232.3 0.1 copy.45
  232.4 0.1 pad_maximum_fusion
  232.5 1.3 copy.46
  233.7 13.8 %all-to-all-start.1 = ((bf16[32,19,512]{2,1,0:T(8,128)(2,1)}), bf16[32,19,512]{2,1,0:T(8,128)(2,1)}, u32[]{:S(2)}, u32[]{:S(2)}) async-start(bf16[32,19,512]{2,1,0:T(8,128)(2,1)} %copy.46), calls=%async_computation.2 | async-start | bytes 1572864 | tf_op jit(solution)/shard_map/all_to_all | solution.py:58
  247.5 44.7 %all-to-all-done.1 = bf16[32,19,512]{2,1,0:T(8,128)(2,1)} async-done(((bf16[32,19,512]{2,1,0:T(8,128)(2,1)}), bf16[32,19,512]{2,1,0:T(8,128)(2,1)}, u32[]{:S(2)}, u32[]{:S(2)}) %all-to-all-start.1) | async-done | bytes 622624 | tf_op jit(solution)/shard_map/all_to_all | solution.py:58
  292.2 2.1 reshape.176
  294.3 3.8 %gather_fusion.1 = bf16[512,512]{1,0:T(8,128)(2,1)} fusion(bf16[576,512]{1,0:T(8,128)(2,1)} %reshape.176, s32[1024]{0:T(1024)S(1)} %pad_clamp_fusion), kind=kCustom, calls=%fused_computation.1 | custom fusion | bytes 1050624 | tf_op jit(solution)/shard_map/gather | solution.py:61
  298.1 2.1 fusion.3
  300.1 0.9 fusion.17
  301.0 0.6 mul.67
  (13 shorter events, 0.1 us)
Async XLA Ops:
  7.2 147.9 %copy-start = (bf16[2,192,4096]{2,1,0:T(8,128)(2,1)S(1)}, bf16[2,192,4096]{2,1,0:T(8,128)(2,1)}, u32[]{:S(2)}) copy-start(bf16[2,192,4096]{2,1,0:T(8,128)(2,1)} %param.15) | copy-start | bytes 9437188
  7.2 7.3 %copy-start.1 = (bf16[64,512]{1,0:T(8,128)(2,1)S(1)}, bf16[64,512]{1,0:T(8,128)(2,1)}, u32[]{:S(2)}) copy-start(bf16[64,512]{1,0:T(8,128)(2,1)} %param.10) | copy-start | bytes 196612
  7.2 142.3 %all-gather.2.cloned.1.call-start = ((), (), s32[]{:S(2)}) async-start(), calls=%async_computation.3 | async-start | bytes 5308416 | tf_op jit(solution)/shard_map/all_gather | solution.py:39
  86.2 0.9 copy-start.2
  90.8 139.8 %reduce-scatter.2.cloned.1.call-start = ((), (), s32[]{:S(2)}) async-start(), calls=%async_computation.4 | async-start | bytes 5308416 | tf_op jit(solution)/shard_map/reduce_scatter | solution.py:48
  233.7 58.5 %all-to-all-start.1 = ((bf16[32,19,512]{2,1,0:T(8,128)(2,1)}), bf16[32,19,512]{2,1,0:T(8,128)(2,1)}, u32[]{:S(2)}, u32[]{:S(2)}) async-start(bf16[32,19,512]{2,1,0:T(8,128)(2,1)} %copy.46), calls=%async_computation.2 | async-start | bytes 1572864 | tf_op jit(solution)/shard_map/all_to_all | solution.py:58
Sparse Core Ops, SparseCore 0:
  91.0 58.4 all-gather.1
  163.4 67.1 reduce-scatter.1

commit v4 on v3

--- a/solution.py
+++ b/solution.py
@@ -42,12 +42,20 @@
     gate = jnp.einsum("erd,edh->erh", rows, w_gate, preferred_element_type=jnp.float32)
     up = jnp.einsum("erd,edh->erh", rows, w_up, preferred_element_type=jnp.float32)
     hidden = (jax.nn.silu(gate) * up).astype(jnp.bfloat16)
-    down = jnp.einsum("erh,ehd->der", hidden, w_down, preferred_element_type=jnp.float32).astype(
-        jnp.bfloat16
-    )
-    summed = lax.psum_scatter(down, "tensor", scatter_dimension=0, tiled=True)
+    splits = lax.axis_size("tensor")
+    w_cols = lax.all_to_all(
+        w_down.reshape(local, w_down.shape[1], splits, feature_cols),
+        "tensor",
+        split_axis=2,
+        concat_axis=1,
+        tiled=True,
+    ).reshape(local, w_down.shape[1] * splits, feature_cols)
+    hidden_all = lax.all_gather(hidden, "tensor", axis=2, tiled=True)
+    expert_out = jnp.einsum(
+        "erh,ehd->erd", hidden_all, w_cols, preferred_element_type=jnp.float32
+    ).astype(jnp.bfloat16)
     back_send = jnp.transpose(
-        summed.reshape(feature_cols, local, owners, capacity), (2, 1, 3, 0)
+        expert_out.reshape(local, owners, capacity, feature_cols), (1, 0, 2, 3)
     ).reshape(owners, local * capacity, feature_cols)
     owner_total = lax.psum(owner_part, "dp")
     total_row = jnp.zeros((owners, 1, feature_cols), jnp.bfloat16)

time: 309 us -> 345 us (1.12)
  waiting for transfers between devices: 161 us -> 183 us
  starting transfers between devices: 13.8 us -> 23.8 us
  local copies, waits for them, and re-layouts: 24.5 us -> 32.8 us
  matrix products: 13.8 us -> 9.06 us
    reduce_scatter x1 -> x0, waiting for transfers between devices: 58 us -> none  [on_device(): summed = lax.psum_scatter(down, 'tensor', scatter_dimension=0, tiled=True)]
    all_gather x1, waiting for transfers between devices: 58.6 us -> 115 us  [on_device(): arrived = lax.all_gather(got, 'tensor', axis=1, tiled=True)]
    all_gather x0 -> x1, waiting for transfers between devices: none -> 23 us  [on_device(): hidden_all = lax.all_gather(hidden, 'tensor', axis=2, tiled=True)]
    all_to_all x0 -> x1, starting transfers between devices: none -> 6.82 us  [on_device(): lax.all_to_all(w_down.reshape(local, w_down.shape[1], splits, feature_col...]
    reshape x0 -> x1, local copies, waits for them, and re-layouts: none -> 3.91 us  [on_device(): w_down.reshape(local, w_down.shape[1], splits, feature_cols)]
    all_to_all x0 -> x1, local copies, waits for them, and re-layouts: none -> 3.85 us  [on_device(): lax.all_to_all(w_down.reshape(local, w_down.shape[1], splits, feature_col...]
    dot_general x1 -> x2, matrix products: 8.21 us -> 5.18 us  [the longest x1 3.76 us: on_device(): jnp.einsum('erh,ehd->erd', hidden_all, w_cols, preferred_element_type=jnp...]
  transfers between devices with their start and end apart: 3 -> 4, of which waited for: 3 -> 3; matrix products, arithmetic and copies ran while one was open for 0% -> 4% of each run, Pallas kernels for 0% -> 0%
where the time goes in v4:
time: 345 us; the launch traced here: 344 us
  waiting for transfers between devices  183 us (53%)
  blocking collectives  73.3 us (21%)
  local copies, waits for them, and re-layouts  32.8 us (10%)
  starting transfers between devices  23.8 us (7%)
  between operations  14.2 us (4%)
  matrix products  9.06 us (3%)
  other arithmetic  7.69 us (2%)
    all_gather x1, waiting for transfers between devices, on_device(): arrived = lax.all_gather(got, 'tensor', axis=1, tiled=True)  115 us
    all_to_all x1, blocking collectives, on_device(): lax.all_to_all(send, 'expert', split_axis=0, concat_axis=0, tiled=True)  64.9 us
    all_to_all x1, waiting for transfers between devices, on_device(): lax.all_to_all(back_send, 'expert', split_axis=0, concat_axis=0, tiled=True)  44.7 us
    all_gather x1, waiting for transfers between devices, on_device(): hidden_all = lax.all_gather(hidden, 'tensor', axis=2, tiled=True)  23 us
    all_to_all x1, starting transfers between devices, on_device(): lax.all_to_all(back_send, 'expert', split_axis=0, concat_axis=0, tiled=True)  16.9 us
    psum x1, blocking collectives, on_device(): owner_total = lax.psum(owner_part, 'dp')  8.41 us
  transfers between devices with their start and end apart: 4, of which 3 were waited for; matrix products, arithmetic and copies ran while one was open for 4% of the time, Pallas kernels for 0%

profile of v4, /device:TPU:1, one launch (start us, length us, event | category | flops | bytes accessed | tf_op | source)
XLA Modules:
  0.0 343.9 jit_solution(12697684734231798757)
XLA Ops:
  7.2 0.8 broadcast_multiply_fusion
  8.1 0.8 copy.55
  8.9 0.1 eq.25
  9.0 0.1 eq.29
  9.1 0.1 copy.54
  9.2 0.1 mul.56
  9.3 1.2 reduce-window.6
  10.5 0.2 slice_reduce_fusion
  10.8 0.1 fusion.10
  10.9 2.4 scatter_custom_fusion
  13.4 0.8 copy.58
  14.2 0.1 mul.58
  14.3 0.1 fusion.12
  14.4 0.1 convert_element_type.63
  14.5 0.1 broadcast_in_dim.29
  14.7 3.2 gather_fusion
  17.9 2.1 gather.9
  20.0 1.3 broadcast_select_fusion
  21.3 0.1 fusion.8
  21.4 64.9 %all_to_all.25 = bf16[32,19,512]{2,1,0:T(8,128)(2,1)S(1)} all-to-all(bf16[32,19,512]{2,1,0:T(8,128)(2,1)S(1)} %fusion.8), channel_id=1, replica_groups=mesh['dp'=4,'expert'=32,'tensor'=8] {'expert'}, dimensions={0} | all-to-all | bytes 1245184 | tf_op jit(solution)/shard_map/all_to_all | solution.py:35
  86.3 0.9 copy-done.2
  87.1 0.2 copy.60
  87.3 1.4 copy.61
  88.7 2.1 reshape.179
  90.9 3.9 %copy.78 = bf16[2,24,8,8,512]{4,3,1,0,2:T(8,128)(2,1)} copy(bf16[2,24,8,8,512]{4,3,2,1,0:T(8,128)(2,1)} %bitcast.42) | data formatting | bytes 6291456 | tf_op jit(solution)/shard_map/reshape | solution.py:47
  94.8 6.8 %all-to-all-start.1 = ((bf16[2,192,8,512]{3,1,0,2:T(8,128)(2,1)}), bf16[2,192,8,512]{3,1,0,2:T(8,128)(2,1)}, u32[]{:S(2)}, u32[]{:S(2)}) async-start(bf16[2,192,8,512]{3,1,0,2:T(8,128)(2,1)} %bitcast.40), calls=%async_computation.1 | async-start | bytes 6291456 | tf_op jit(solution)/shard_map/all_to_all | solution.py:46
  101.6 0.0 all-gather.5.cloned.1.call-start
  101.7 115.2 %all-gather.3.cloned.1.call-done = bf16[576,4096]{1,0:T(8,128)(2,1)} async-done(((bf16[576,512]{1,0:T(8,128)(2,1)}), bf16[576,4096]{1,0:T(8,128)(2,1)}) %all-gather.3.cloned.1.call-update) | async-done | bytes 4718608 | tf_op jit(solution)/shard_map/all_gather | solution.py:39
  216.9 3.9 %fusion.22 = f32[2,288,192]{2,1,0:T(8,128)S(1)} fusion(bf16[2,288,4096]{2,1,0:T(8,128)(2,1)} %bitcast.50, bf16[2,4096,192]{1,2,0:T(8,128)(2,1)S(1)} %copy-done), kind=kOutput, calls=%fused_computation.48 | convolution fusion | flops 905969664 | bytes 8306688 | tf_op jit(solution)/shard_map/erd,edh->erh/dot_general | solution.py:42
  220.8 0.8 copy-done.4
  221.7 1.4 fusion.6
  223.1 0.9 copy.62
  224.0 0.9 fusion.16
  224.9 8.4 %psum.7 = bf16[2]{0:T(256)(128)(2,1)S(1)} all-reduce(f32[2]{0:T(128)S(1)} %fusion.16), channel_id=1, replica_groups=mesh['dp'=4,'expert'=32,'tensor'=8] {'dp'}, use_global_device_ids=true, to_apply=%region_6.7 | all-reduce | flops 2 | bytes 12 | tf_op jit(solution)/shard_map/psum | solution.py:60
  233.3 3.8 %copy.64 = bf16[2,8,192,1,512]{4,2,1,0,3:T(8,128)(2,1)} copy(bf16[2,8,192,1,512]{4,2,0,1,3:T(8,128)(2,1)} %bitcast.7) | data formatting | bytes 6291456 | tf_op jit(solution)/shard_map/all_to_all | solution.py:46
  237.2 23.0 %all-gather.5.cloned.1.call-done = bf16[2,288,1536]{1,0,2:T(2,128)(2,1)} async-done(((bf16[2,288,192]{1,0,2:T(2,128)(2,1)}), bf16[2,288,1536]{1,0,2:T(2,128)(2,1)}) %all-gather.5.cloned.1.call-update) | async-done | bytes 1769488 | tf_op jit(solution)/shard_map/all_gather | solution.py:53
  260.2 3.8 %fusion.3 = bf16[2,288,512]{2,1,0:T(8,128)(2,1)S(1)} fusion(bf16[2,1536,512]{2,1,0:T(8,128)(2,1)} %bitcast.43, bf16[2,288,1536]{1,0,2:T(2,128)(2,1)} %all-gather.5.cloned.1.call-done), kind=kOutput, calls=%fused_computation.8 | convolution fusion | flops 906264576 | bytes 5505024 | tf_op jit(solution)/shard_map/erh,ehd->erd/dot_general | solution.py:54
  263.9 0.6 copy.66
  264.6 0.1 copy.67
  264.7 0.1 pad_maximum_fusion
  264.7 1.3 copy.68
  266.0 16.9 %all-to-all-start.2 = ((bf16[32,19,512]{2,1,0:T(8,128)(2,1)}), bf16[32,19,512]{2,1,0:T(8,128)(2,1)}, u32[]{:S(2)}, u32[]{:S(2)}) async-start(bf16[32,19,512]{2,1,0:T(8,128)(2,1)} %copy.68), calls=%async_computation.2 | async-start | bytes 1572864 | tf_op jit(solution)/shard_map/all_to_all | solution.py:66
  282.9 44.7 %all-to-all-done.2 = bf16[32,19,512]{2,1,0:T(8,128)(2,1)} async-done(((bf16[32,19,512]{2,1,0:T(8,128)(2,1)}), bf16[32,19,512]{2,1,0:T(8,128)(2,1)}, u32[]{:S(2)}, u32[]{:S(2)}) %all-to-all-start.2) | async-done | bytes 622624 | tf_op jit(solution)/shard_map/all_to_all | solution.py:66
  327.6 0.9 fusion.15
  328.5 0.6 mul.67
  329.1 2.1 reshape.185
  331.2 3.8 %gather_fusion.1 = bf16[512,512]{1,0:T(8,128)(2,1)} fusion(bf16[576,512]{1,0:T(8,128)(2,1)} %reshape.185, s32[1024]{0:T(1024)S(1)} %pad_clamp_fusion), kind=kCustom, calls=%fused_computation.1 | custom fusion | bytes 1050624 | tf_op jit(solution)/shard_map/gather | solution.py:69
  335.0 2.1 fusion.7
  (23 shorter events, 0.2 us)
Async XLA Ops:
  7.2 209.7 %copy-start = (bf16[2,4096,192]{1,2,0:T(8,128)(2,1)S(1)}, bf16[2,4096,192]{1,2,0:T(8,128)(2,1)}, u32[]{:S(2)}) copy-start(bf16[2,4096,192]{1,2,0:T(8,128)(2,1)} %param.13) | copy-start | bytes 9437188
  7.2 7.5 %copy-start.1 = (bf16[64,512]{1,0:T(8,128)(2,1)S(1)}, bf16[64,512]{1,0:T(8,128)(2,1)}, u32[]{:S(2)}) copy-start(bf16[64,512]{1,0:T(8,128)(2,1)} %param.10) | copy-start | bytes 196612
  7.2 209.7 %all-gather.3.cloned.1.call-start = ((), (), s32[]{:S(2)}) async-start(), calls=%async_computation.3 | async-start | bytes 5308416 | tf_op jit(solution)/shard_map/all_gather | solution.py:39
  86.3 0.9 copy-start.2
  94.8 138.5 %all-to-all-start.1 = ((bf16[2,192,8,512]{3,1,0,2:T(8,128)(2,1)}), bf16[2,192,8,512]{3,1,0,2:T(8,128)(2,1)}, u32[]{:S(2)}, u32[]{:S(2)}) async-start(bf16[2,192,8,512]{3,1,0,2:T(8,128)(2,1)} %bitcast.40), calls=%async_computation.1 | async-start | bytes 6291456 | tf_op jit(solution)/shard_map/all_to_all | solution.py:46
  101.6 158.6 %all-gather.5.cloned.1.call-start = ((), (), s32[]{:S(2)}) async-start(), calls=%async_computation.4 | async-start | bytes 2654208 | tf_op jit(solution)/shard_map/all_gather | solution.py:53
  216.9 3.9 %copy-start.3 = (bf16[576,4096]{1,0:T(8,128)(2,1)S(1)}, bf16[576,4096]{1,0:T(8,128)(2,1)}, u32[]{:S(2)}) copy-start(bf16[576,4096]{1,0:T(8,128)(2,1)} %all-gather.3.cloned.1.call-done) | copy-start | bytes 14155780
  216.9 4.7 %copy-start.4 = (bf16[2,4096,192]{1,2,0:T(8,128)(2,1)S(1)}, bf16[2,4096,192]{1,2,0:T(8,128)(2,1)}, u32[]{:S(2)}) copy-start(bf16[2,4096,192]{1,2,0:T(8,128)(2,1)} %param.14) | copy-start | bytes 9437188
  266.0 61.6 %all-to-all-start.2 = ((bf16[32,19,512]{2,1,0:T(8,128)(2,1)}), bf16[32,19,512]{2,1,0:T(8,128)(2,1)}, u32[]{:S(2)}, u32[]{:S(2)}) async-start(bf16[32,19,512]{2,1,0:T(8,128)(2,1)} %copy.68), calls=%async_computation.2 | async-start | bytes 1572864 | tf_op jit(solution)/shard_map/all_to_all | solution.py:66
Sparse Core Ops, SparseCore 0:
  91.0 125.8 all-gather.2
  224.1 35.9 all-gather.4

commit v5 on v4

--- a/solution.py
+++ b/solution.py
@@ -36,23 +36,32 @@
     owner_part = jnp.sum(got[:, local * capacity, :local].astype(jnp.float32), axis=0)
     got = got[:, : local * capacity].reshape(owners, local, capacity, feature_cols)
     got = jnp.transpose(got, (1, 0, 2, 3)).reshape(local * owners * capacity, feature_cols)
+    splits = lax.axis_size("tensor")
+    me = lax.axis_index("tensor")
+    hid_block = w_down.shape[1]
+    w_blocks = w_down.reshape(local, hid_block, splits, feature_cols)
+    received = []
+    for shift in range(splits):
+        block = lax.dynamic_index_in_dim(w_blocks, (me + shift) % splits, axis=2, keepdims=False)
+        if shift:
+            block = lax.ppermute(
+                block, "tensor", [(j, (j + shift) % splits) for j in range(splits)]
+            )
+        received.append(block)
+    w_cols = jnp.stack(received, axis=1)
+    got, w_cols = lax.optimization_barrier((got, w_cols))
     arrived = lax.all_gather(got, "tensor", axis=1, tiled=True)
     model_width = arrived.shape[1]
     rows = arrived.reshape(local, owners * capacity, model_width)
     gate = jnp.einsum("erd,edh->erh", rows, w_gate, preferred_element_type=jnp.float32)
     up = jnp.einsum("erd,edh->erh", rows, w_up, preferred_element_type=jnp.float32)
     hidden = (jax.nn.silu(gate) * up).astype(jnp.bfloat16)
-    splits = lax.axis_size("tensor")
-    w_cols = lax.all_to_all(
-        w_down.reshape(local, w_down.shape[1], splits, feature_cols),
-        "tensor",
-        split_axis=2,
-        concat_axis=1,
-        tiled=True,
-    ).reshape(local, w_down.shape[1] * splits, feature_cols)
     hidden_all = lax.all_gather(hidden, "tensor", axis=2, tiled=True)
+    hidden_all = hidden_all.reshape(local, owners * capacity, splits, hid_block)
+    order = (me - jnp.arange(splits, dtype=jnp.int32)) % splits
+    hidden_all = jnp.take(hidden_all, order, axis=2)
     expert_out = jnp.einsum(
-        "erh,ehd->erd", hidden_all, w_cols, preferred_element_type=jnp.float32
+        "ersh,eshd->erd", hidden_all, w_cols, preferred_element_type=jnp.float32
     ).astype(jnp.bfloat16)
     back_send = jnp.transpose(
         expert_out.reshape(local, owners, capacity, feature_cols), (1, 0, 2, 3)

time: 345 us -> 370 us (1.072)
  blocking collectives: 73.3 us -> 8.42 us
  starting transfers between devices: 23.8 us -> 72.2 us
  local copies, waits for them, and re-layouts: 32.8 us -> 64.7 us
  waiting for transfers between devices: 183 us -> 192 us
    all_to_all x1 -> x0, blocking collectives: 64.9 us -> none  [on_device(): lax.all_to_all(send, 'expert', split_axis=0, concat_axis=0, tiled=True)]
    all_gather x1, waiting for transfers between devices: 115 us -> 66.1 us  [on_device(): arrived = lax.all_gather(got, 'tensor', axis=1, tiled=True)]
    ppermute x0 -> x7, waiting for transfers between devices: none -> 44.1 us  [on_device(): lax.ppermute(block, 'tensor', [(j, (j + shift) % splits) for j in range(s...]
    ppermute x0 -> x7, starting transfers between devices: none -> 34.6 us  [on_device(): lax.ppermute(block, 'tensor', [(j, (j + shift) % splits) for j in range(s...]
    dynamic_slice x0 -> x1, local copies, waits for them, and re-layouts: none -> 17.5 us  [on_device(): lax.dynamic_index_in_dim(w_blocks, (me + shift) % splits, axis=2, keepdim...]
    all_to_all x1, starting transfers between devices: 6.82 us -> 20.5 us  [on_device(): lax.all_to_all(send, 'expert', split_axis=0, concat_axis=0, tiled=True)]
    all_gather x1, waiting for transfers between devices: 23 us -> 36.6 us  [on_device(): hidden_all = lax.all_gather(hidden, 'tensor', axis=2, tiled=True)]
    unnamed x12 -> x25, local copies, waits for them, and re-layouts: 3.35 us -> 13.4 us
  transfers between devices with their start and end apart: 4 -> 11, of which waited for: 3 -> 7; matrix products, arithmetic and copies ran while one was open for 4% -> 8% of each run, Pallas kernels for 0% -> 0%
where the time goes in v5:
time: 370 us; the launch traced here: 369 us
  waiting for transfers between devices  192 us (52%)
  starting transfers between devices  72.2 us (20%)
  local copies, waits for them, and re-layouts  64.7 us (17%)
  between operations  14.5 us (4%)
  matrix products  9.1 us (2%)
  other arithmetic  8.61 us (2%)
  blocking collectives  8.42 us (2%)
    all_gather x1, waiting for transfers between devices, on_device(): arrived = lax.all_gather(got, 'tensor', axis=1, tiled=True)  66.1 us
    all_to_all x1, waiting for transfers between devices, on_device(): lax.all_to_all(back_send, 'expert', split_axis=0, concat_axis=0, tiled=True)  44.7 us
    ppermute x7, waiting for transfers between devices, on_device(): lax.ppermute(block, 'tensor', [(j, (j + shift) % splits) for j in range(s...  44.1 us
    all_gather x1, waiting for transfers between devices, on_device(): hidden_all = lax.all_gather(hidden, 'tensor', axis=2, tiled=True)  36.6 us
    ppermute x7, starting transfers between devices, on_device(): lax.ppermute(block, 'tensor', [(j, (j + shift) % splits) for j in range(s...  34.6 us
    all_to_all x1, starting transfers between devices, on_device(): lax.all_to_all(send, 'expert', split_axis=0, concat_axis=0, tiled=True)  20.5 us
    dynamic_slice x1, local copies, waits for them, and re-layouts, on_device(): lax.dynamic_index_in_dim(w_blocks, (me + shift) % splits, axis=2, keepdim...  17.5 us
    all_to_all x1, starting transfers between devices, on_device(): lax.all_to_all(back_send, 'expert', split_axis=0, concat_axis=0, tiled=True)  16.9 us
  transfers between devices with their start and end apart: 11, of which 7 were waited for; matrix products, arithmetic and copies ran while one was open for 8% of the time, Pallas kernels for 0%

profile of v5, /device:TPU:1, one launch (start us, length us, event | category | flops | bytes accessed | tf_op | source)
XLA Modules:
  0.0 369.1 jit_solution(15993733398718764483)
XLA Ops:
  7.2 0.8 broadcast_multiply_fusion
  8.0 0.9 copy.54
  9.3 1.2 reduce-window.6
  10.9 2.4 scatter_custom_fusion
  14.7 3.2 gather_fusion
  17.9 2.1 gather.13
  20.0 1.3 broadcast_select_fusion
  21.3 1.0 fusion.14
  22.3 20.5 %all-to-all-start = ((bf16[32,19,512]{2,1,0:T(8,128)(2,1)}), bf16[32,19,512]{2,1,0:T(8,128)(2,1)}, u32[]{:S(2)}, u32[]{:S(2)}) async-start(bf16[32,19,512]{2,1,0:T(8,128)(2,1)} %fusion.14), calls=%async_computation | async-start | bytes 1572864 | tf_op jit(solution)/shard_map/all_to_all | solution.py:35
  42.9 5.0 %copy.79 = bf16[48,8,8,512]{3,2,1,0:T(8,128)(2,1)} copy(bf16[48,8,8,512]{3,1,2,0:T(8,128)(2,1)} %bitcast.88) | data formatting | bytes 6291456
  47.9 17.5 %constant_dynamic-slice_fusion = (bf16[2,192,1,512]{3,2,1,0:T(2,128)(2,1)S(1)}, bf16[2,192,1,512]{3,2,1,0:T(2,128)(2,1)S(1)}, bf16[2,192,1,512]{3,2,1,0:T(2,128)...) fusion(bf16[2,192,8,512]{3,2,1,0:T(8,128)(2,1)} %bitcast.87, ...), kind=kLoop, calls=%fused_computation.73 | loop fusion | bytes 6291488 | tf_op jit(solution)/shard_map/jit(dynamic_index_in_dim)/dynamic_slice | solution.py:45
  65.4 3.2 collective-permute-start
  68.7 4.2 %collective-permute-start.1 = (bf16[2,192,512]{2,1,0:T(8,128)(2,1)S(1)}, bf16[2,192,512]{2,1,0:T(8,128)(2,1)S(1)}, u32[]{:S(2)}, u32[]{:S(2)}) collective-permute-start(bf16[2,192,512]{2,1,0:T(8,128)(2,1)S(1)} %bitcast.98), channel_id=1, source_target_pairs={{0,2},{1,3},{2,4},{3,5},{4,6},{5,7},{6,0},{7,1},{8,10},{9,11},{10,... | collective-permute-start | bytes 1179656 | tf_op jit(solution)/shard_map/ppermute | solution.py:47
  73.0 4.6 %collective-permute-start.2 = (bf16[2,192,512]{2,1,0:T(8,128)(2,1)S(1)}, bf16[2,192,512]{2,1,0:T(8,128)(2,1)S(1)}, u32[]{:S(2)}, u32[]{:S(2)}) collective-permute-start(bf16[2,192,512]{2,1,0:T(8,128)(2,1)S(1)} %bitcast.97), channel_id=1, source_target_pairs={{0,3},{1,4},{2,5},{3,6},{4,7},{5,0},{6,1},{7,2},{8,11},{9,12},{10,... | collective-permute-start | bytes 1179656 | tf_op jit(solution)/shard_map/ppermute | solution.py:47
  77.7 3.5 collective-permute-start.3
  81.3 4.9 %collective-permute-start.4 = (bf16[2,192,512]{2,1,0:T(8,128)(2,1)S(1)}, bf16[2,192,512]{2,1,0:T(8,128)(2,1)S(1)}, u32[]{:S(2)}, u32[]{:S(2)}) collective-permute-start(bf16[2,192,512]{2,1,0:T(8,128)(2,1)S(1)} %bitcast.94), channel_id=1, source_target_pairs={{0,5},{1,6},{2,7},{3,0},{4,1},{5,2},{6,3},{7,4},{8,13},{9,14},{10,... | collective-permute-start | bytes 1179656 | tf_op jit(solution)/shard_map/ppermute | solution.py:47
  86.3 0.8 bitcast_dynamic-update-slice_fusion
  87.1 5.0 %collective-permute-start.5 = (bf16[2,192,512]{2,1,0:T(8,128)(2,1)S(1)}, bf16[2,192,512]{2,1,0:T(8,128)(2,1)S(1)}, u32[]{:S(2)}, u32[]{:S(2)}) collective-permute-start(bf16[2,192,512]{2,1,0:T(8,128)(2,1)S(1)} %bitcast.96), channel_id=1, source_target_pairs={{0,6},{1,7},{2,0},{3,1},{4,2},{5,3},{6,4},{7,5},{8,14},{9,15},{10,... | collective-permute-start | bytes 1179656 | tf_op jit(solution)/shard_map/ppermute | solution.py:47
  92.1 0.8 bitcast_dynamic-update-slice_fusion.7
  92.9 9.1 %collective-permute-start.6 = (bf16[2,192,512]{2,1,0:T(8,128)(2,1)S(1)}, bf16[2,192,512]{2,1,0:T(8,128)(2,1)S(1)}, u32[]{:S(2)}, u32[]{:S(2)}) collective-permute-start(bf16[2,192,512]{2,1,0:T(8,128)(2,1)S(1)} %bitcast.93), channel_id=1, source_target_pairs={{0,7},{1,0},{2,1},{3,2},{4,3},{5,4},{6,5},{7,6},{8,15},{9,8},{10,9... | collective-permute-start | bytes 1179656 | tf_op jit(solution)/shard_map/ppermute | solution.py:47
  102.0 0.8 bitcast_dynamic-update-slice_fusion.6
  102.8 16.8 %collective-permute-done.2 = bf16[2,192,512]{2,1,0:T(8,128)(2,1)S(1)} collective-permute-done((bf16[2,192,512]{2,1,0:T(8,128)(2,1)S(1)}, bf16[2,192,512]{2,1,0:T(8,128)(2,1)S(1)}, u32[]{:S(2)}, u32[]{:S(2)}) %collective-permute-start.2) | collective-permute-done | bytes 393248 | tf_op jit(solution)/shard_map/ppermute | solution.py:47
  120.4 11.5 %collective-permute-done.3 = bf16[2,192,512]{2,1,0:T(8,128)(2,1)S(1)} collective-permute-done((bf16[2,192,512]{2,1,0:T(8,128)(2,1)S(1)}, bf16[2,192,512]{2,1,0:T(8,128)(2,1)S(1)}, u32[]{:S(2)}, u32[]{:S(2)}) %collective-permute-start.3) | collective-permute-done | bytes 393248 | tf_op jit(solution)/shard_map/ppermute | solution.py:47
  131.9 0.8 bitcast_dynamic-update-slice_fusion.4
  132.7 0.8 bitcast_dynamic-update-slice_fusion.3
  133.5 10.9 %collective-permute-done.5 = bf16[2,192,512]{2,1,0:T(8,128)(2,1)S(1)} collective-permute-done((bf16[2,192,512]{2,1,0:T(8,128)(2,1)S(1)}, bf16[2,192,512]{2,1,0:T(8,128)(2,1)S(1)}, u32[]{:S(2)}, u32[]{:S(2)}) %collective-permute-start.5) | collective-permute-done | bytes 393248 | tf_op jit(solution)/shard_map/ppermute | solution.py:47
  145.2 4.9 %collective-permute-done.6 = bf16[2,192,512]{2,1,0:T(8,128)(2,1)S(1)} collective-permute-done((bf16[2,192,512]{2,1,0:T(8,128)(2,1)S(1)}, bf16[2,192,512]{2,1,0:T(8,128)(2,1)S(1)}, u32[]{:S(2)}, u32[]{:S(2)}) %collective-permute-start.6) | collective-permute-done | bytes 393248 | tf_op jit(solution)/shard_map/ppermute | solution.py:47
  150.9 1.3 copy.59
  152.2 1.4 copy.60
  153.5 2.2 reshape.233
  156.0 66.1 %all-gather.3.cloned.1.call-done = bf16[576,4096]{1,0:T(8,128)(2,1)} async-done(((bf16[576,512]{1,0:T(8,128)(2,1)}), bf16[576,4096]{1,0:T(8,128)(2,1)}) %all-gather.3.cloned.1.call-update) | async-done | bytes 4718608 | tf_op jit(solution)/shard_map/all_gather | solution.py:53
  222.1 3.9 %fusion.32 = f32[2,288,192]{2,1,0:T(8,128)S(1)} fusion(bf16[2,288,4096]{2,1,0:T(8,128)(2,1)} %bitcast.103, bf16[2,4096,192]{1,2,0:T(8,128)(2,1)S(1)} %copy-done), kind=kOutput, calls=%fused_computation.89 | convolution fusion | flops 905969664 | bytes 8306688 | tf_op jit(solution)/shard_map/erd,edh->erh/dot_general | solution.py:56
  226.0 0.8 copy-done.3
  226.9 1.4 fusion.11
  228.3 0.9 copy.61
  229.3 0.9 fusion.22
  230.2 8.4 %psum.7 = bf16[2]{0:T(256)(128)(2,1)S(1)} all-reduce(f32[2]{0:T(128)S(1)} %fusion.22), channel_id=1, replica_groups=mesh['dp'=4,'expert'=32,'tensor'=8] {'dp'}, use_global_device_ids=true, to_apply=%region_6.7 | all-reduce | flops 2 | bytes 12 | tf_op jit(solution)/shard_map/psum | solution.py:69
  238.6 36.6 %all-gather.5.cloned.1.call-done = bf16[2,288,1536]{1,0,2:T(2,128)(2,1)} async-done(((bf16[2,288,192]{1,0,2:T(2,128)(2,1)}), bf16[2,288,1536]{1,0,2:T(2,128)(2,1)}) %all-gather.5.cloned.1.call-update) | async-done | bytes 1769488 | tf_op jit(solution)/shard_map/all_gather | solution.py:59
  275.2 6.4 %copy.63 = bf16[2,288,8,192]{3,1,2,0:T(8,128)(2,1)} copy(bf16[2,288,8,192]{1,0,3,2:T(2,128)(2,1)} %bitcast.89) | data formatting | bytes 3538944 | tf_op jit(solution)/shard_map/reshape | solution.py:60
  281.6 3.8 %gather_fusion.1 = bf16[8,2,288,192]{3,2,1,0:T(8,128)(2,1)} fusion(bf16[2,288,8,192]{3,1,2,0:T(8,128)(2,1)} %copy.63, s32[1024]{0:T(1024)S(1)} %pad_clamp_fusion.1), kind=kCustom, calls=%fused_computation.1 | custom fusion | bytes 3538976 | tf_op jit(solution)/shard_map/jit(_take)/gather | solution.py:62
  285.4 3.8 %fusion.8 = bf16[2,288,512]{2,1,0:T(8,128)(2,1)S(1)} fusion(bf16[2,8,192,512]{3,2,0,1:T(8,128)(2,1)} %bitcast_dynamic-update-slice_fusion.1, bf16[8,2,288,192]{3,2,1,0:T(8,128)(2,1)} %gather_fusion.1, pred[8]{0:T(512)(128)(4,1)S(1)} %compare_and_fusion), kind=kOutput, calls=%fused_computation.11 | convolution fusion | flops 907149312 | bytes 5505032 | tf_op jit(solution)/shard_map/ersh,eshd->erd/dot_general | solution.py:63
  289.9 1.3 copy.66
  291.2 16.9 %all-to-all-start.1 = ((bf16[32,19,512]{2,1,0:T(8,128)(2,1)}), bf16[32,19,512]{2,1,0:T(8,128)(2,1)}, u32[]{:S(2)}, u32[]{:S(2)}) async-start(bf16[32,19,512]{2,1,0:T(8,128)(2,1)} %copy.66), calls=%async_computation.1 | async-start | bytes 1572864 | tf_op jit(solution)/shard_map/all_to_all | solution.py:75
  308.1 44.7 %all-to-all-done.1 = bf16[32,19,512]{2,1,0:T(8,128)(2,1)} async-done(((bf16[32,19,512]{2,1,0:T(8,128)(2,1)}), bf16[32,19,512]{2,1,0:T(8,128)(2,1)}, u32[]{:S(2)}, u32[]{:S(2)}) %all-to-all-start.1) | async-done | bytes 622624 | tf_op jit(solution)/shard_map/all_to_all | solution.py:75
  352.8 0.9 fusion.21
  354.4 2.1 reshape.239
  356.4 3.8 %gather_fusion.2 = bf16[512,512]{1,0:T(8,128)(2,1)} fusion(bf16[576,512]{1,0:T(8,128)(2,1)} %reshape.239, s32[1024]{0:T(1024)S(1)} %pad_clamp_fusion), kind=kCustom, calls=%fused_computation.2 | custom fusion | bytes 1050624 | tf_op jit(solution)/shard_map/gather | solution.py:78
  360.2 2.1 fusion.13
  (54 shorter events, 6.5 us)
Async XLA Ops:
  7.2 215.0 %copy-start = (bf16[2,4096,192]{1,2,0:T(8,128)(2,1)S(1)}, bf16[2,4096,192]{1,2,0:T(8,128)(2,1)}, u32[]{:S(2)}) copy-start(bf16[2,4096,192]{1,2,0:T(8,128)(2,1)} %param.13) | copy-start | bytes 9437188
  7.2 7.5 %copy-start.1 = (bf16[64,512]{1,0:T(8,128)(2,1)S(1)}, bf16[64,512]{1,0:T(8,128)(2,1)}, u32[]{:S(2)}) copy-start(bf16[64,512]{1,0:T(8,128)(2,1)} %param.10) | copy-start | bytes 196612
  22.3 128.6 %all-to-all-start = ((bf16[32,19,512]{2,1,0:T(8,128)(2,1)}), bf16[32,19,512]{2,1,0:T(8,128)(2,1)}, u32[]{:S(2)}, u32[]{:S(2)}) async-start(bf16[32,19,512]{2,1,0:T(8,128)(2,1)} %fusion.14), calls=%async_computation | async-start | bytes 1572864 | tf_op jit(solution)/shard_map/all_to_all | solution.py:35
  42.7 179.4 %all-gather.3.cloned.1.call-start = ((), (), s32[]{:S(2)}) async-start(), calls=%async_computation.2 | async-start | bytes 5308416 | tf_op jit(solution)/shard_map/all_gather | solution.py:53
  65.4 21.7 %collective-permute-start = (bf16[2,192,512]{2,1,0:T(8,128)(2,1)S(1)}, bf16[2,192,512]{2,1,0:T(8,128)(2,1)S(1)}, u32[]{:S(2)}, u32[]{:S(2)}) collective-permute-start(bf16[2,192,512]{2,1,0:T(8,128)(2,1)S(1)} %bitcast.99), channel_id=1, source_target_pairs={{0,1},{1,2},{2,3},{3,4},{4,5},{5,6},{6,7},{7,0},{8,9},{9,10},{10,1... | collective-permute-start | bytes 1179656 | tf_op jit(solution)/shard_map/ppermute | solution.py:47
  68.7 24.2 %collective-permute-start.1 = (bf16[2,192,512]{2,1,0:T(8,128)(2,1)S(1)}, bf16[2,192,512]{2,1,0:T(8,128)(2,1)S(1)}, u32[]{:S(2)}, u32[]{:S(2)}) collective-permute-start(bf16[2,192,512]{2,1,0:T(8,128)(2,1)S(1)} %bitcast.98), channel_id=1, source_target_pairs={{0,2},{1,3},{2,4},{3,5},{4,6},{5,7},{6,0},{7,1},{8,10},{9,11},{10,... | collective-permute-start | bytes 1179656 | tf_op jit(solution)/shard_map/ppermute | solution.py:47
  73.0 46.6 %collective-permute-start.2 = (bf16[2,192,512]{2,1,0:T(8,128)(2,1)S(1)}, bf16[2,192,512]{2,1,0:T(8,128)(2,1)S(1)}, u32[]{:S(2)}, u32[]{:S(2)}) collective-permute-start(bf16[2,192,512]{2,1,0:T(8,128)(2,1)S(1)} %bitcast.97), channel_id=1, source_target_pairs={{0,3},{1,4},{2,5},{3,6},{4,7},{5,0},{6,1},{7,2},{8,11},{9,12},{10,... | collective-permute-start | bytes 1179656 | tf_op jit(solution)/shard_map/ppermute | solution.py:47
  77.7 54.2 %collective-permute-start.3 = (bf16[2,192,512]{2,1,0:T(8,128)(2,1)S(1)}, bf16[2,192,512]{2,1,0:T(8,128)(2,1)S(1)}, u32[]{:S(2)}, u32[]{:S(2)}) collective-permute-start(bf16[2,192,512]{2,1,0:T(8,128)(2,1)S(1)} %bitcast.95), channel_id=1, source_target_pairs={{0,4},{1,5},{2,6},{3,7},{4,0},{5,1},{6,2},{7,3},{8,12},{9,13},{10,... | collective-permute-start | bytes 1179656 | tf_op jit(solution)/shard_map/ppermute | solution.py:47
  81.3 51.4 %collective-permute-start.4 = (bf16[2,192,512]{2,1,0:T(8,128)(2,1)S(1)}, bf16[2,192,512]{2,1,0:T(8,128)(2,1)S(1)}, u32[]{:S(2)}, u32[]{:S(2)}) collective-permute-start(bf16[2,192,512]{2,1,0:T(8,128)(2,1)S(1)} %bitcast.94), channel_id=1, source_target_pairs={{0,5},{1,6},{2,7},{3,0},{4,1},{5,2},{6,3},{7,4},{8,13},{9,14},{10,... | collective-permute-start | bytes 1179656 | tf_op jit(solution)/shard_map/ppermute | solution.py:47
  87.1 57.3 %collective-permute-start.5 = (bf16[2,192,512]{2,1,0:T(8,128)(2,1)S(1)}, bf16[2,192,512]{2,1,0:T(8,128)(2,1)S(1)}, u32[]{:S(2)}, u32[]{:S(2)}) collective-permute-start(bf16[2,192,512]{2,1,0:T(8,128)(2,1)S(1)} %bitcast.96), channel_id=1, source_target_pairs={{0,6},{1,7},{2,0},{3,1},{4,2},{5,3},{6,4},{7,5},{8,14},{9,15},{10,... | collective-permute-start | bytes 1179656 | tf_op jit(solution)/shard_map/ppermute | solution.py:47
  92.9 57.2 %collective-permute-start.6 = (bf16[2,192,512]{2,1,0:T(8,128)(2,1)S(1)}, bf16[2,192,512]{2,1,0:T(8,128)(2,1)S(1)}, u32[]{:S(2)}, u32[]{:S(2)}) collective-permute-start(bf16[2,192,512]{2,1,0:T(8,128)(2,1)S(1)} %bitcast.93), channel_id=1, source_target_pairs={{0,7},{1,0},{2,1},{3,2},{4,3},{5,4},{6,5},{7,6},{8,15},{9,8},{10,9... | collective-permute-start | bytes 1179656 | tf_op jit(solution)/shard_map/ppermute | solution.py:47
  155.8 119.4 %all-gather.5.cloned.1.call-start = ((), (), s32[]{:S(2)}) async-start(), calls=%async_computation.3 | async-start | bytes 2654208 | tf_op jit(solution)/shard_map/all_gather | solution.py:59
  222.1 3.9 %copy-start.2 = (bf16[576,4096]{1,0:T(8,128)(2,1)S(1)}, bf16[576,4096]{1,0:T(8,128)(2,1)}, u32[]{:S(2)}) copy-start(bf16[576,4096]{1,0:T(8,128)(2,1)} %all-gather.3.cloned.1.call-done) | copy-start | bytes 14155780
  222.1 4.7 %copy-start.3 = (bf16[2,4096,192]{1,2,0:T(8,128)(2,1)S(1)}, bf16[2,4096,192]{1,2,0:T(8,128)(2,1)}, u32[]{:S(2)}) copy-start(bf16[2,4096,192]{1,2,0:T(8,128)(2,1)} %param.14) | copy-start | bytes 9437188
  291.2 61.6 %all-to-all-start.1 = ((bf16[32,19,512]{2,1,0:T(8,128)(2,1)}), bf16[32,19,512]{2,1,0:T(8,128)(2,1)}, u32[]{:S(2)}, u32[]{:S(2)}) async-start(bf16[32,19,512]{2,1,0:T(8,128)(2,1)} %copy.66), calls=%async_computation.1 | async-start | bytes 1572864 | tf_op jit(solution)/shard_map/all_to_all | solution.py:75
Sparse Core Ops, SparseCore 0:
  155.9 66.1 all-gather.2
  229.3 45.7 all-gather.4

commit v6 on v3

--- a/solution.py
+++ b/solution.py
@@ -15,15 +15,13 @@
     onehot = (flat_ids[:, None] == jnp.arange(experts, dtype=jnp.int32)[None, :]).astype(jnp.int32)
     ranks = jnp.sum((jnp.cumsum(onehot, axis=0) - onehot) * onehot, axis=1)
     target = flat_ids * capacity + ranks
-    pair_count = flat_ids.shape[0]
-    source = (
-        jnp.full((experts * capacity,), -1, jnp.int32)
-        .at[target]
-        .set(jnp.arange(pair_count, dtype=jnp.int32) // chosen)
+    slot_ids = jnp.arange(experts * capacity, dtype=jnp.int32)
+    slot_of_token = jnp.any(
+        (target[None, :] == slot_ids[:, None]).reshape(experts * capacity, tok_rows, chosen), axis=2
     )
-    filled = (source >= 0)[:, None]
-    safe = jnp.maximum(source, 0)
-    outgoing = jnp.where(filled, tokens[safe], jnp.zeros((), jnp.bfloat16))
+    outgoing = jnp.dot(
+        slot_of_token.astype(jnp.bfloat16), tokens, preferred_element_type=jnp.float32
+    ).astype(jnp.bfloat16)
     outgoing = outgoing.reshape(owners, local, capacity, feature_cols)
     group_load = jnp.sum(onehot.astype(jnp.float32) * combine_weight.reshape(-1)[:, None], axis=0)
     load_row = jnp.zeros((owners, 1, feature_cols), jnp.bfloat16)
@@ -42,12 +40,14 @@
     gate = jnp.einsum("erd,edh->erh", rows, w_gate, preferred_element_type=jnp.float32)
     up = jnp.einsum("erd,edh->erh", rows, w_up, preferred_element_type=jnp.float32)
     hidden = (jax.nn.silu(gate) * up).astype(jnp.bfloat16)
-    down = jnp.einsum("erh,ehd->der", hidden, w_down, preferred_element_type=jnp.float32).astype(
+    down = jnp.einsum("erh,ehd->erd", hidden, w_down, preferred_element_type=jnp.float32).astype(
         jnp.bfloat16
     )
-    summed = lax.psum_scatter(down, "tensor", scatter_dimension=0, tiled=True)
+    summed = lax.psum_scatter(
+        down.reshape(local * owners * capacity, model_width), "tensor", scatter_dimension=1, tiled=True
+    )
     back_send = jnp.transpose(
-        summed.reshape(feature_cols, local, owners, capacity), (2, 1, 3, 0)
+        summed.reshape(local, owners, capacity, feature_cols), (1, 0, 2, 3)
     ).reshape(owners, local * capacity, feature_cols)
     owner_total = lax.psum(owner_part, "dp")
     total_row = jnp.zeros((owners, 1, feature_cols), jnp.bfloat16)
@@ -58,9 +58,18 @@
     back = lax.all_to_all(back_send, "expert", split_axis=0, concat_axis=0, tiled=True)
     total_load = back[:, local * capacity, :local].astype(jnp.float32).reshape(experts)
     back = back[:, : local * capacity].reshape(experts * capacity, feature_cols)
-    picked = back[target].astype(jnp.float32)
-    weighted = picked * combine_weight.reshape(-1)[:, None]
-    mixed = jnp.sum(weighted.reshape(tok_rows, chosen, feature_cols), axis=1).astype(jnp.bfloat16)
+    weight_of_slot = jnp.sum(
+        jnp.where(
+            target[:, None] == slot_ids[None, :], combine_weight.reshape(-1)[:, None], 0.0
+        ).reshape(tok_rows, chosen, experts * capacity),
+        axis=1,
+    )
+    mixed = jnp.dot(
+        weight_of_slot,
+        back.astype(jnp.float32),
+        precision=lax.Precision.HIGHEST,
+        preferred_element_type=jnp.float32,
+    ).astype(jnp.bfloat16)
     all_tokens = tok_rows * lax.axis_size("dp") * owners
     expert_load = total_load * (experts / all_tokens)
     return (mixed, expert_load)

time: 309 us -> 304 us (0.984)
  local copies, waits for them, and re-layouts: 24.5 us -> 17 us
  matrix products: 13.8 us -> 17.9 us
    gather x3 -> x0, local copies, waits for them, and re-layouts: 9.1 us -> none  [the longest x2 5.31 us: on_device(): outgoing = jnp.where(filled, tokens[safe], jnp.zeros((), jnp.bfloat16))]
    dot_general x1 -> x3, matrix products: 8.21 us -> 12.4 us  [the longest x1 8.2 us: on_device(): jnp.einsum('erh,ehd->erd', hidden, w_down, preferred_element_type=jnp.flo...]
where the time goes in v6:
time: 304 us; the launch traced here: 303 us
  waiting for transfers between devices  161 us (53%)
  blocking collectives  73.3 us (24%)
  matrix products  17.9 us (6%)
  local copies, waits for them, and re-layouts  17 us (6%)
  between operations  14.1 us (5%)
  starting transfers between devices  13.8 us (5%)
  other arithmetic  6.23 us (2%)
    all_to_all x1, blocking collectives, on_device(): lax.all_to_all(send, 'expert', split_axis=0, concat_axis=0, tiled=True)  64.9 us
    all_gather x1, waiting for transfers between devices, on_device(): arrived = lax.all_gather(got, 'tensor', axis=1, tiled=True)  58.6 us
    reduce_scatter x1, waiting for transfers between devices, on_device(): lax.psum_scatter(down.reshape(local * owners * capacity, model_width), 't...  58 us
    all_to_all x1, waiting for transfers between devices, on_device(): lax.all_to_all(back_send, 'expert', split_axis=0, concat_axis=0, tiled=True)  44.2 us
    all_to_all x1, starting transfers between devices, on_device(): lax.all_to_all(back_send, 'expert', split_axis=0, concat_axis=0, tiled=True)  13.7 us
    psum x1, blocking collectives, on_device(): owner_total = lax.psum(owner_part, 'dp')  8.42 us
    dot_general x1, matrix products, on_device(): jnp.einsum('erh,ehd->erd', hidden, w_down, preferred_element_type=jnp.flo...  8.2 us
  transfers between devices with their start and end apart: 3, of which 3 were waited for; matrix products, arithmetic and copies ran while one was open for 0% of the time, Pallas kernels for 0%

profile of v6, /device:TPU:1, one launch (start us, length us, event | category | flops | bytes accessed | tf_op | source)
XLA Modules:
  0.0 303.3 jit_solution(13989482542464097337)
XLA Ops:
  7.2 0.0 copy-start
  7.2 0.0 all-gather.2.cloned.1.call-start
  7.2 0.9 copy.61
  8.1 0.1 eq.53
  8.2 0.1 eq.57
  8.3 0.8 copy.66
  9.1 0.1 broadcast_in_dim.12
  9.2 0.1 fusion.13
  9.3 0.1 convert_element_type.59
  9.5 1.2 reduce-window.6
  10.7 0.2 slice_reduce_fusion
  10.9 0.1 fusion.11
  11.1 0.1 reduce_sum.39
  11.2 0.1 copy.64
  11.2 0.7 multiply_add_fusion
  11.9 0.1 copy.65
  12.0 0.5 fusion.1
  12.5 2.0 convolution_convert_fusion.1
  14.5 2.1 reshape_reshape.3
  16.6 1.2 fusion.3
  17.8 64.9 %all_to_all.10 = bf16[32,19,512]{2,1,0:T(8,128)(2,1)S(1)} all-to-all(bf16[32,19,512]{2,1,0:T(8,128)(2,1)S(1)} %fusion.3), channel_id=1, replica_groups=mesh['dp'=4,'expert'=32,'tensor'=8] {'expert'}, dimensions={0} | all-to-all | bytes 1245184 | tf_op jit(solution)/shard_map/all_to_all | solution.py:33
  82.7 0.0 copy-start.1
  82.7 0.9 copy-done.1
  83.6 0.2 copy.70
  83.8 1.4 copy.71
  85.1 2.2 reshape.170
  87.3 0.0 all-gather.2.cloned.1.call-update
  87.3 0.0 reduce-scatter.2.cloned.1.call-start
  87.4 58.6 %all-gather.2.cloned.1.call-done = bf16[576,4096]{1,0:T(8,128)(2,1)} async-done(((bf16[576,512]{1,0:T(8,128)(2,1)}), bf16[576,4096]{1,0:T(8,128)(2,1)}) %all-gather.2.cloned.1.call-update) | async-done | bytes 4718608 | tf_op jit(solution)/shard_map/all_gather | solution.py:37
  146.0 5.6 %fusion.19 = f32[2,288,192]{2,1,0:T(8,128)} fusion(bf16[2,288,4096]{2,1,0:T(8,128)(2,1)} %bitcast.34, bf16[2,4096,192]{1,2,0:T(8,128)(2,1)} %param.13), kind=kOutput, calls=%fused_computation.38 | convolution fusion | flops 905969664 | bytes 8306688 | tf_op jit(solution)/shard_map/erd,edh->erh/dot_general | solution.py:40
  151.5 0.0 copy-done
  151.5 8.2 %convolution_convert_fusion = bf16[2,288,4096]{2,1,0:T(8,128)(2,1)} fusion(bf16[2,192,4096]{2,1,0:T(8,128)(2,1)S(1)} %copy-done, bf16[2,288,4096]{2,1,0:T(8,128)(2,1)} %bitcast.35, bf16[2,4096,192]{1,2,0:T(8,128)(2,1)} %param.14, f32[2,288,192]{2,1,0:T(8,128)} %fusion.19), kind=kOutput, calls=%fused_computation | convolution fusion | flops 1814962176 | bytes 16171008 | tf_op jit(solution)/shard_map/erh,ehd->erd/dot_general | solution.py:43
  159.7 0.0 reduce-scatter.2.cloned.1.call-update
  159.8 0.9 fusion.17
  160.7 8.4 %psum.7 = bf16[2]{0:T(256)(128)(2,1)S(1)} all-reduce(f32[2]{0:T(128)S(1)} %fusion.17), channel_id=1, replica_groups=mesh['dp'=4,'expert'=32,'tensor'=8] {'dp'}, use_global_device_ids=true, to_apply=%region_8.9 | all-reduce | flops 2 | bytes 12 | tf_op jit(solution)/shard_map/psum | solution.py:52
  169.1 58.0 %reduce-scatter.2.cloned.1.call-done = bf16[576,512]{1,0:T(8,128)(2,1)} async-done(((bf16[576,4096]{1,0:T(8,128)(2,1)}), bf16[576,512]{1,0:T(8,128)(2,1)}) %reduce-scatter.2.cloned.1.call-update) | async-done | bytes 589840 | tf_op jit(solution)/shard_map/reduce_scatter | solution.py:46
  227.1 2.2 reshape.173
  229.3 1.6 copy.72
  230.9 0.1 pad_maximum_fusion
  231.0 1.3 copy.73
  232.2 13.7 %all-to-all-start.1 = ((bf16[32,19,512]{2,1,0:T(8,128)(2,1)}), bf16[32,19,512]{2,1,0:T(8,128)(2,1)}, u32[]{:S(2)}, u32[]{:S(2)}) async-start(bf16[32,19,512]{2,1,0:T(8,128)(2,1)} %copy.73), calls=%async_computation.2 | async-start | bytes 1572864 | tf_op jit(solution)/shard_map/all_to_all | solution.py:58
  246.0 0.5 select_reduce_fusion
  246.5 44.2 %all-to-all-done.1 = bf16[32,19,512]{2,1,0:T(8,128)(2,1)} async-done(((bf16[32,19,512]{2,1,0:T(8,128)(2,1)}), bf16[32,19,512]{2,1,0:T(8,128)(2,1)}, u32[]{:S(2)}, u32[]{:S(2)}) %all-to-all-start.1) | async-done | bytes 622624 | tf_op jit(solution)/shard_map/all_to_all | solution.py:58
  290.7 0.9 fusion.16
  291.6 0.6 mul.50
  292.2 2.1 reshape.175
  294.3 2.1 convolution_convert_fusion.2
  (5 shorter events, 0.1 us)
Async XLA Ops:
  7.2 144.4 %copy-start = (bf16[2,192,4096]{2,1,0:T(8,128)(2,1)S(1)}, bf16[2,192,4096]{2,1,0:T(8,128)(2,1)}, u32[]{:S(2)}) copy-start(bf16[2,192,4096]{2,1,0:T(8,128)(2,1)} %param.15) | copy-start | bytes 9437188
  7.2 138.8 %all-gather.2.cloned.1.call-start = ((), (), s32[]{:S(2)}) async-start(), calls=%async_computation.3 | async-start | bytes 5308416 | tf_op jit(solution)/shard_map/all_gather | solution.py:37
  82.7 0.9 copy-start.1
  87.3 139.8 %reduce-scatter.2.cloned.1.call-start = ((), (), s32[]{:S(2)}) async-start(), calls=%async_computation.4 | async-start | bytes 5308416 | tf_op jit(solution)/shard_map/reduce_scatter | solution.py:46
  232.2 58.5 %all-to-all-start.1 = ((bf16[32,19,512]{2,1,0:T(8,128)(2,1)}), bf16[32,19,512]{2,1,0:T(8,128)(2,1)}, u32[]{:S(2)}, u32[]{:S(2)}) async-start(bf16[32,19,512]{2,1,0:T(8,128)(2,1)} %copy.73), calls=%async_computation.2 | async-start | bytes 1572864 | tf_op jit(solution)/shard_map/all_to_all | solution.py:58
Sparse Core Ops, SparseCore 0:
  87.5 58.4 all-gather.1
  159.9 67.1 reduce-scatter.1

commit v7 on v6

--- a/solution.py
+++ b/solution.py
@@ -30,7 +30,9 @@
     send = jnp.concatenate(
         [outgoing.reshape(owners, local * capacity, feature_cols), load_row], axis=1
     )
-    got = lax.all_to_all(send, "expert", split_axis=0, concat_axis=0, tiled=True)
+    got = lax.all_to_all(
+        send.reshape(owners, -1, 128), "expert", split_axis=0, concat_axis=0, tiled=True
+    ).reshape(send.shape)
     owner_part = jnp.sum(got[:, local * capacity, :local].astype(jnp.float32), axis=0)
     got = got[:, : local * capacity].reshape(owners, local, capacity, feature_cols)
     got = jnp.transpose(got, (1, 0, 2, 3)).reshape(local * owners * capacity, feature_cols)
@@ -55,7 +57,9 @@
         jnp.broadcast_to(owner_total.astype(jnp.bfloat16)[None, :], (owners, local))
     )
     back_send = jnp.concatenate([back_send, total_row], axis=1)
-    back = lax.all_to_all(back_send, "expert", split_axis=0, concat_axis=0, tiled=True)
+    back = lax.all_to_all(
+        back_send.reshape(owners, -1, 128), "expert", split_axis=0, concat_axis=0, tiled=True
+    ).reshape(back_send.shape)
     total_load = back[:, local * capacity, :local].astype(jnp.float32).reshape(experts)
     back = back[:, : local * capacity].reshape(experts * capacity, feature_cols)
     weight_of_slot = jnp.sum(

time: 304 us -> 303 us (level)
  local copies, waits for them, and re-layouts: 17 us -> 26.1 us
  waiting for transfers between devices: 161 us -> 155 us
  blocking collectives: 73.3 us -> 68 us
    reshape x0 -> x4, local copies, waits for them, and re-layouts: none -> 8.89 us  [the longest x1 2.25 us: on_device(): back_send.reshape(owners, -1, 128)]
    all_to_all x1, waiting for transfers between devices: 44.2 us -> 38.7 us  [on_device(): lax.all_to_all(back_send.reshape(owners, -1, 128), 'expert', split_axis=0...]
    all_to_all x1, blocking collectives: 64.9 us -> 59.6 us  [on_device(): lax.all_to_all(send.reshape(owners, -1, 128), 'expert', split_axis=0, con...]
where the time goes in v7:
time: 303 us; the launch traced here: 302 us
  waiting for transfers between devices  155 us (51%)
  blocking collectives  68 us (22%)
  local copies, waits for them, and re-layouts  26.1 us (9%)
  matrix products  17.9 us (6%)
  between operations  14.1 us (5%)
  starting transfers between devices  13.8 us (5%)
  other arithmetic  7.14 us (2%)
    all_to_all x1, blocking collectives, on_device(): lax.all_to_all(send.reshape(owners, -1, 128), 'expert', split_axis=0, con...  59.6 us
    all_gather x1, waiting for transfers between devices, on_device(): arrived = lax.all_gather(got, 'tensor', axis=1, tiled=True)  58.5 us
    reduce_scatter x1, waiting for transfers between devices, on_device(): lax.psum_scatter(down.reshape(local * owners * capacity, model_width), 't...  58 us
    all_to_all x1, waiting for transfers between devices, on_device(): lax.all_to_all(back_send.reshape(owners, -1, 128), 'expert', split_axis=0...  38.7 us
    all_to_all x1, starting transfers between devices, on_device(): lax.all_to_all(back_send.reshape(owners, -1, 128), 'expert', split_axis=0...  13.7 us
    psum x1, blocking collectives, on_device(): owner_total = lax.psum(owner_part, 'dp')  8.41 us
    dot_general x1, matrix products, on_device(): jnp.einsum('erh,ehd->erd', hidden, w_down, preferred_element_type=jnp.flo...  8.21 us
  transfers between devices with their start and end apart: 3, of which 3 were waited for; matrix products, arithmetic and copies ran while one was open for 0% of the time, Pallas kernels for 0%

profile of v7, /device:TPU:1, one launch (start us, length us, event | category | flops | bytes accessed | tf_op | source)
XLA Modules:
  0.0 302.4 jit_solution(15078021996534479308)
XLA Ops:
  7.2 0.0 copy-start
  7.2 0.0 all-gather.2.cloned.1.call-start
  7.2 0.9 copy.36
  8.1 0.1 eq.53
  8.2 0.1 eq.57
  8.3 0.8 copy.41
  9.1 0.1 broadcast_in_dim.12
  9.2 0.1 fusion.13
  9.3 0.1 convert_element_type.59
  9.5 1.2 reduce-window.6
  10.7 0.2 slice_reduce_fusion
  10.9 0.1 fusion.11
  11.1 0.1 reduce_sum.39
  11.2 0.1 copy.39
  11.2 0.7 multiply_add_fusion
  11.9 0.1 copy.40
  12.0 0.5 fusion.1
  12.5 2.0 convolution_convert_fusion.1
  14.5 2.1 reshape_reshape.3
  16.6 2.1 fusion.3
  18.7 2.2 reshape.181
  21.0 59.6 %all_to_all.10 = bf16[32,76,128]{2,1,0:T(8,128)(2,1)} all-to-all(bf16[32,76,128]{2,1,0:T(8,128)(2,1)} %reshape.181), channel_id=1, replica_groups=mesh['dp'=4,'expert'=32,'tensor'=8] {'expert'}, dimensions={0} | all-to-all | bytes 1245184 | tf_op jit(solution)/shard_map/all_to_all | solution.py:33
  80.6 2.2 reshape.182
  82.8 1.3 copy.45
  84.1 1.4 copy.46
  85.5 2.2 reshape.184
  87.6 0.0 all-gather.2.cloned.1.call-update
  87.6 0.0 reduce-scatter.2.cloned.1.call-start
  87.7 58.5 %all-gather.2.cloned.1.call-done = bf16[576,4096]{1,0:T(8,128)(2,1)} async-done(((bf16[576,512]{1,0:T(8,128)(2,1)}), bf16[576,4096]{1,0:T(8,128)(2,1)}) %all-gather.2.cloned.1.call-update) | async-done | bytes 4718608 | tf_op jit(solution)/shard_map/all_gather | solution.py:39
  146.2 5.6 %fusion.19 = f32[2,288,192]{2,1,0:T(8,128)} fusion(bf16[2,288,4096]{2,1,0:T(8,128)(2,1)} %bitcast.35, bf16[2,4096,192]{1,2,0:T(8,128)(2,1)} %param.13), kind=kOutput, calls=%fused_computation.38 | convolution fusion | flops 905969664 | bytes 8306688 | tf_op jit(solution)/shard_map/erd,edh->erh/dot_general | solution.py:42
  151.8 8.2 %convolution_convert_fusion = bf16[2,288,4096]{2,1,0:T(8,128)(2,1)} fusion(bf16[2,192,4096]{2,1,0:T(8,128)(2,1)S(1)} %copy-done, bf16[2,288,4096]{2,1,0:T(8,128)(2,1)} %bitcast.36, bf16[2,4096,192]{1,2,0:T(8,128)(2,1)} %param.14, f32[2,288,192]{2,1,0:T(8,128)} %fusion.19), kind=kOutput, calls=%fused_computation | convolution fusion | flops 1814962176 | bytes 16171008 | tf_op jit(solution)/shard_map/erh,ehd->erd/dot_general | solution.py:45
  160.0 0.0 reduce-scatter.2.cloned.1.call-update
  160.0 0.9 fusion.17
  160.9 8.4 %psum.7 = bf16[2]{0:T(256)(128)(2,1)S(1)} all-reduce(f32[2]{0:T(128)S(1)} %fusion.17), channel_id=1, replica_groups=mesh['dp'=4,'expert'=32,'tensor'=8] {'dp'}, use_global_device_ids=true, to_apply=%region_8.9 | all-reduce | flops 2 | bytes 12 | tf_op jit(solution)/shard_map/psum | solution.py:54
  169.3 58.0 %reduce-scatter.2.cloned.1.call-done = bf16[576,512]{1,0:T(8,128)(2,1)} async-done(((bf16[576,4096]{1,0:T(8,128)(2,1)}), bf16[576,512]{1,0:T(8,128)(2,1)}) %reduce-scatter.2.cloned.1.call-update) | async-done | bytes 589840 | tf_op jit(solution)/shard_map/reduce_scatter | solution.py:48
  227.4 2.2 reshape.187
  229.6 1.6 copy.47
  231.2 0.1 pad_maximum_fusion
  231.2 1.2 copy.48
  232.5 2.3 reshape.189
  234.7 13.7 %all-to-all-start.1 = ((bf16[32,76,128]{2,1,0:T(8,128)(2,1)}), bf16[32,76,128]{2,1,0:T(8,128)(2,1)}, u32[]{:S(2)}, u32[]{:S(2)}) async-start(bf16[32,76,128]{2,1,0:T(8,128)(2,1)} %reshape.189), calls=%async_computation.2 | async-start | bytes 1310720 | tf_op jit(solution)/shard_map/all_to_all | solution.py:60
  248.4 0.5 select_reduce_fusion
  248.9 38.7 %all-to-all-done.1 = bf16[32,76,128]{2,1,0:T(8,128)(2,1)} async-done(((bf16[32,76,128]{2,1,0:T(8,128)(2,1)}), bf16[32,76,128]{2,1,0:T(8,128)(2,1)}, u32[]{:S(2)}, u32[]{:S(2)}) %all-to-all-start.1) | async-done | bytes 622624 | tf_op jit(solution)/shard_map/all_to_all | solution.py:60
  287.6 2.2 reshape.190
  289.8 0.9 fusion.16
  290.7 0.6 mul.50
  291.3 2.1 reshape.191
  293.4 2.1 convolution_convert_fusion.2
  (6 shorter events, 0.1 us)
Async XLA Ops:
  7.2 144.6 %copy-start = (bf16[2,192,4096]{2,1,0:T(8,128)(2,1)S(1)}, bf16[2,192,4096]{2,1,0:T(8,128)(2,1)}, u32[]{:S(2)}) copy-start(bf16[2,192,4096]{2,1,0:T(8,128)(2,1)} %param.15) | copy-start | bytes 9437188
  7.2 139.0 %all-gather.2.cloned.1.call-start = ((), (), s32[]{:S(2)}) async-start(), calls=%async_computation.3 | async-start | bytes 5308416 | tf_op jit(solution)/shard_map/all_gather | solution.py:39
  87.6 139.7 %reduce-scatter.2.cloned.1.call-start = ((), (), s32[]{:S(2)}) async-start(), calls=%async_computation.4 | async-start | bytes 5308416 | tf_op jit(solution)/shard_map/reduce_scatter | solution.py:48
  234.7 52.9 %all-to-all-start.1 = ((bf16[32,76,128]{2,1,0:T(8,128)(2,1)}), bf16[32,76,128]{2,1,0:T(8,128)(2,1)}, u32[]{:S(2)}, u32[]{:S(2)}) async-start(bf16[32,76,128]{2,1,0:T(8,128)(2,1)} %reshape.189), calls=%async_computation.2 | async-start | bytes 1310720 | tf_op jit(solution)/shard_map/all_to_all | solution.py:60
Sparse Core Ops, SparseCore 0:
  87.8 58.3 all-gather.1
  160.1 67.1 reduce-scatter.1

commit v8 on v6

--- a/solution.py
+++ b/solution.py
@@ -24,15 +24,16 @@
     ).astype(jnp.bfloat16)
     outgoing = outgoing.reshape(owners, local, capacity, feature_cols)
     group_load = jnp.sum(onehot.astype(jnp.float32) * combine_weight.reshape(-1)[:, None], axis=0)
-    load_row = jnp.zeros((owners, 1, feature_cols), jnp.bfloat16)
+    lanes = 128
+    per_row = feature_cols // lanes
+    data_rows = local * capacity * per_row
+    load_row = jnp.zeros((owners, per_row, lanes), jnp.bfloat16)
     load_row = load_row.at[:, 0, :local].set(group_load.reshape(owners, local).astype(jnp.bfloat16))
 
-    send = jnp.concatenate(
-        [outgoing.reshape(owners, local * capacity, feature_cols), load_row], axis=1
-    )
+    send = jnp.concatenate([outgoing.reshape(owners, data_rows, lanes), load_row], axis=1)
     got = lax.all_to_all(send, "expert", split_axis=0, concat_axis=0, tiled=True)
-    owner_part = jnp.sum(got[:, local * capacity, :local].astype(jnp.float32), axis=0)
-    got = got[:, : local * capacity].reshape(owners, local, capacity, feature_cols)
+    owner_part = jnp.sum(got[:, data_rows, :local].astype(jnp.float32), axis=0)
+    got = got[:, :data_rows].reshape(owners, local, capacity * per_row, lanes)
     got = jnp.transpose(got, (1, 0, 2, 3)).reshape(local * owners * capacity, feature_cols)
     arrived = lax.all_gather(got, "tensor", axis=1, tiled=True)
     model_width = arrived.shape[1]
@@ -47,17 +48,17 @@
         down.reshape(local * owners * capacity, model_width), "tensor", scatter_dimension=1, tiled=True
     )
     back_send = jnp.transpose(
-        summed.reshape(local, owners, capacity, feature_cols), (1, 0, 2, 3)
-    ).reshape(owners, local * capacity, feature_cols)
+        summed.reshape(local, owners, capacity * per_row, lanes), (1, 0, 2, 3)
+    ).reshape(owners, data_rows, lanes)
     owner_total = lax.psum(owner_part, "dp")
-    total_row = jnp.zeros((owners, 1, feature_cols), jnp.bfloat16)
+    total_row = jnp.zeros((owners, per_row, lanes), jnp.bfloat16)
     total_row = total_row.at[:, 0, :local].set(
         jnp.broadcast_to(owner_total.astype(jnp.bfloat16)[None, :], (owners, local))
     )
     back_send = jnp.concatenate([back_send, total_row], axis=1)
     back = lax.all_to_all(back_send, "expert", split_axis=0, concat_axis=0, tiled=True)
-    total_load = back[:, local * capacity, :local].astype(jnp.float32).reshape(experts)
-    back = back[:, : local * capacity].reshape(experts * capacity, feature_cols)
+    total_load = back[:, data_rows, :local].astype(jnp.float32).reshape(experts)
+    back = back[:, :data_rows].reshape(experts * capacity, feature_cols)
     weight_of_slot = jnp.sum(
         jnp.where(
             target[:, None] == slot_ids[None, :], combine_weight.reshape(-1)[:, None], 0.0

time: 304 us -> 294 us (0.967)
  waiting for transfers between devices: 161 us -> 155 us
  blocking collectives: 73.3 us -> 67.7 us
    all_to_all x1, blocking collectives: 64.9 us -> 59.3 us  [on_device(): lax.all_to_all(send, 'expert', split_axis=0, concat_axis=0, tiled=True)]
    all_to_all x1, waiting for transfers between devices: 44.2 us -> 38.7 us  [on_device(): lax.all_to_all(back_send, 'expert', split_axis=0, concat_axis=0, tiled=True)]
where the time goes in v8:
time: 294 us; the launch traced here: 293 us
  waiting for transfers between devices  155 us (53%)
  blocking collectives  67.7 us (23%)
  local copies, waits for them, and re-layouts  18.3 us (6%)
  matrix products  17.9 us (6%)
  between operations  14.1 us (5%)
  starting transfers between devices  13.8 us (5%)
  other arithmetic  6.11 us (2%)
    all_to_all x1, blocking collectives, on_device(): lax.all_to_all(send, 'expert', split_axis=0, concat_axis=0, tiled=True)  59.3 us
    all_gather x1, waiting for transfers between devices, on_device(): arrived = lax.all_gather(got, 'tensor', axis=1, tiled=True)  58.5 us
    reduce_scatter x1, waiting for transfers between devices, on_device(): lax.psum_scatter(down.reshape(local * owners * capacity, model_width), 't...  58 us
    all_to_all x1, waiting for transfers between devices, on_device(): lax.all_to_all(back_send, 'expert', split_axis=0, concat_axis=0, tiled=True)  38.7 us
    all_to_all x1, starting transfers between devices, on_device(): lax.all_to_all(back_send, 'expert', split_axis=0, concat_axis=0, tiled=True)  13.8 us
    psum x1, blocking collectives, on_device(): owner_total = lax.psum(owner_part, 'dp')  8.4 us
    dot_general x1, matrix products, on_device(): jnp.einsum('erh,ehd->erd', hidden, w_down, preferred_element_type=jnp.flo...  8.21 us
  transfers between devices with their start and end apart: 3, of which 3 were waited for; matrix products, arithmetic and copies ran while one was open for 0% of the time, Pallas kernels for 0%

profile of v8, /device:TPU:1, one launch (start us, length us, event | category | flops | bytes accessed | tf_op | source)
XLA Modules:
  0.0 293.3 jit_solution(9680435943149866801)
XLA Ops:
  7.2 0.0 copy-start
  7.2 0.0 all-gather.2.cloned.1.call-start
  7.2 0.9 copy.59
  8.1 0.1 eq.53
  8.2 0.1 eq.57
  8.3 0.8 copy.64
  9.1 0.1 broadcast_in_dim.12
  9.2 0.1 fusion.13
  9.3 0.1 convert_element_type.59
  9.5 1.2 reduce-window.6
  10.7 0.2 slice_reduce_fusion
  10.9 0.1 fusion.11
  11.1 0.1 reduce_sum.39
  11.2 0.1 copy.62
  11.2 0.7 multiply_add_fusion
  11.9 0.1 copy.63
  12.0 0.5 fusion
  12.5 2.0 convolution_convert_fusion.1
  14.5 2.2 reshape_reshape.3
  16.7 1.1 fusion.3
  17.8 59.3 %all_to_all.10 = bf16[32,76,128]{2,1,0:T(8,128)(2,1)S(1)} all-to-all(bf16[32,76,128]{2,1,0:T(8,128)(2,1)S(1)} %fusion.3), channel_id=1, replica_groups=mesh['dp'=4,'expert'=32,'tensor'=8] {'expert'}, dimensions={0} | all-to-all | bytes 1245184 | tf_op jit(solution)/shard_map/all_to_all | solution.py:34
  77.1 0.0 copy-start.1
  77.1 0.8 copy-done.1
  78.0 0.1 copy.72
  78.1 1.1 copy.69
  79.2 2.3 reshape.173
  81.5 0.0 all-gather.2.cloned.1.call-update
  81.5 0.0 reduce-scatter.2.cloned.1.call-start
  81.5 58.5 %all-gather.2.cloned.1.call-done = bf16[576,4096]{1,0:T(8,128)(2,1)} async-done(((bf16[576,512]{1,0:T(8,128)(2,1)}), bf16[576,4096]{1,0:T(8,128)(2,1)}) %all-gather.2.cloned.1.call-update) | async-done | bytes 4718608 | tf_op jit(solution)/shard_map/all_gather | solution.py:38
  140.0 5.5 %fusion.19 = f32[2,288,192]{2,1,0:T(8,128)} fusion(bf16[2,288,4096]{2,1,0:T(8,128)(2,1)} %bitcast.35, bf16[2,4096,192]{1,2,0:T(8,128)(2,1)} %param.13), kind=kOutput, calls=%fused_computation.39 | convolution fusion | flops 905969664 | bytes 8306688 | tf_op jit(solution)/shard_map/erd,edh->erh/dot_general | solution.py:41
  145.6 0.0 copy-done
  145.6 8.2 %convolution_convert_fusion = bf16[2,288,4096]{2,1,0:T(8,128)(2,1)} fusion(bf16[2,192,4096]{2,1,0:T(8,128)(2,1)S(1)} %copy-done, bf16[2,288,4096]{2,1,0:T(8,128)(2,1)} %bitcast.36, bf16[2,4096,192]{1,2,0:T(8,128)(2,1)} %param.14, f32[2,288,192]{2,1,0:T(8,128)} %fusion.19), kind=kOutput, calls=%fused_computation | convolution fusion | flops 1814962176 | bytes 16171008 | tf_op jit(solution)/shard_map/erh,ehd->erd/dot_general | solution.py:44
  153.8 0.0 reduce-scatter.2.cloned.1.call-update
  153.8 0.9 fusion.17
  154.7 8.4 %psum.7 = bf16[2]{0:T(256)(128)(2,1)S(1)} all-reduce(f32[2]{0:T(128)S(1)} %fusion.17), channel_id=1, replica_groups=mesh['dp'=4,'expert'=32,'tensor'=8] {'dp'}, use_global_device_ids=true, to_apply=%region_8.9 | all-reduce | flops 2 | bytes 12 | tf_op jit(solution)/shard_map/psum | solution.py:53
  163.1 58.0 %reduce-scatter.2.cloned.1.call-done = bf16[576,512]{1,0:T(8,128)(2,1)} async-done(((bf16[576,4096]{1,0:T(8,128)(2,1)}), bf16[576,512]{1,0:T(8,128)(2,1)}) %reduce-scatter.2.cloned.1.call-update) | async-done | bytes 589840 | tf_op jit(solution)/shard_map/reduce_scatter | solution.py:47
  221.2 2.3 reshape.176
  223.4 1.2 copy.70
  224.6 0.1 pad_maximum_fusion
  224.7 1.1 copy.71
  225.8 13.8 %all-to-all-start.1 = ((bf16[32,76,128]{2,1,0:T(8,128)(2,1)}), bf16[32,76,128]{2,1,0:T(8,128)(2,1)}, u32[]{:S(2)}, u32[]{:S(2)}) async-start(bf16[32,76,128]{2,1,0:T(8,128)(2,1)} %copy.71), calls=%async_computation.2 | async-start | bytes 1310720 | tf_op jit(solution)/shard_map/all_to_all | solution.py:59
  239.6 0.5 select_reduce_fusion
  240.0 38.7 %all-to-all-done.1 = bf16[32,76,128]{2,1,0:T(8,128)(2,1)} async-done(((bf16[32,76,128]{2,1,0:T(8,128)(2,1)}), bf16[32,76,128]{2,1,0:T(8,128)(2,1)}, u32[]{:S(2)}, u32[]{:S(2)}) %all-to-all-start.1) | async-done | bytes 622624 | tf_op jit(solution)/shard_map/all_to_all | solution.py:59
  278.7 0.9 fusion.16
  279.6 0.6 mul.50
  280.2 1.9 slice.73
  282.1 2.2 reshape.179
  284.3 2.1 convolution_convert_fusion.2
  (6 shorter events, 0.1 us)
Async XLA Ops:
  7.2 138.4 %copy-start = (bf16[2,192,4096]{2,1,0:T(8,128)(2,1)S(1)}, bf16[2,192,4096]{2,1,0:T(8,128)(2,1)}, u32[]{:S(2)}) copy-start(bf16[2,192,4096]{2,1,0:T(8,128)(2,1)} %param.15) | copy-start | bytes 9437188
  7.2 132.9 %all-gather.2.cloned.1.call-start = ((), (), s32[]{:S(2)}) async-start(), calls=%async_computation.3 | async-start | bytes 5308416 | tf_op jit(solution)/shard_map/all_gather | solution.py:38
  77.1 0.8 copy-start.1
  81.5 139.7 %reduce-scatter.2.cloned.1.call-start = ((), (), s32[]{:S(2)}) async-start(), calls=%async_computation.4 | async-start | bytes 5308416 | tf_op jit(solution)/shard_map/reduce_scatter | solution.py:47
  225.8 52.9 %all-to-all-start.1 = ((bf16[32,76,128]{2,1,0:T(8,128)(2,1)}), bf16[32,76,128]{2,1,0:T(8,128)(2,1)}, u32[]{:S(2)}, u32[]{:S(2)}) async-start(bf16[32,76,128]{2,1,0:T(8,128)(2,1)} %copy.71), calls=%async_computation.2 | async-start | bytes 1310720 | tf_op jit(solution)/shard_map/all_to_all | solution.py:59
Sparse Core Ops, SparseCore 0:
  81.6 58.3 all-gather.1
  153.9 67.1 reduce-scatter.1

commit v9 on v8

--- a/solution.py
+++ b/solution.py
@@ -58,19 +58,26 @@
     back_send = jnp.concatenate([back_send, total_row], axis=1)
     back = lax.all_to_all(back_send, "expert", split_axis=0, concat_axis=0, tiled=True)
     total_load = back[:, data_rows, :local].astype(jnp.float32).reshape(experts)
-    back = back[:, :data_rows].reshape(experts * capacity, feature_cols)
     weight_of_slot = jnp.sum(
         jnp.where(
             target[:, None] == slot_ids[None, :], combine_weight.reshape(-1)[:, None], 0.0
         ).reshape(tok_rows, chosen, experts * capacity),
         axis=1,
     )
-    mixed = jnp.dot(
-        weight_of_slot,
+    lane_group = jnp.arange(per_row, dtype=jnp.int32)
+    spread = jnp.where(
+        lane_group[:, None, None, None, None] == lane_group[None, None, None, None, :],
+        weight_of_slot.reshape(1, tok_rows, owners, local * capacity, 1),
+        0.0,
+    ).reshape(per_row, tok_rows, owners, data_rows)
+    spread = jnp.pad(spread, ((0, 0), (0, 0), (0, 0), (0, back.shape[1] - data_rows)))
+    mixed = jnp.einsum(
+        "qtoj,ojl->tql",
+        spread,
         back.astype(jnp.float32),
         precision=lax.Precision.HIGHEST,
         preferred_element_type=jnp.float32,
-    ).astype(jnp.bfloat16)
+    ).reshape(tok_rows, feature_cols).astype(jnp.bfloat16)
     all_tokens = tok_rows * lax.axis_size("dp") * owners
     expert_load = total_load * (experts / all_tokens)
     return (mixed, expert_load)

time: 294 us -> 294 us (level)
  waiting for transfers between devices: 155 us -> 145 us
  other arithmetic: 6.11 us -> 10.7 us
  matrix products: 17.9 us -> 21.2 us
    all_to_all x1, waiting for transfers between devices: 38.7 us -> 28.9 us  [on_device(): lax.all_to_all(back_send, 'expert', split_axis=0, concat_axis=0, tiled=True)]
    broadcast_in_dim x1 -> x6, local copies, waits for them, and re-layouts: 0.09 us -> 5.17 us  [on_device(): jnp.where(lane_group[:, None, None, None, None] == lane_group[None, None,...]
    select_n x0 -> x1, other arithmetic: none -> 3.71 us  [on_device(): jnp.where(lane_group[:, None, None, None, None] == lane_group[None, None,...]
    dot_general x1, matrix products: 2.13 us -> 5.45 us  [on_device(): jnp.einsum('qtoj,ojl->tql', spread, back.astype(jnp.float32), precision=l...]
  transfers between devices with their start and end apart: 3 -> 3, of which waited for: 3 -> 3; matrix products, arithmetic and copies ran while one was open for 0% -> 4% of each run, Pallas kernels for 0% -> 0%
where the time goes in v9:
time: 294 us; the launch traced here: 293 us
  waiting for transfers between devices  145 us (49%)
  blocking collectives  67.7 us (23%)
  matrix products  21.2 us (7%)
  local copies, waits for them, and re-layouts  20 us (7%)
  between operations  14.2 us (5%)
  starting transfers between devices  13.8 us (5%)
  other arithmetic  10.7 us (4%)
    all_to_all x1, blocking collectives, on_device(): lax.all_to_all(send, 'expert', split_axis=0, concat_axis=0, tiled=True)  59.3 us
    all_gather x1, waiting for transfers between devices, on_device(): arrived = lax.all_gather(got, 'tensor', axis=1, tiled=True)  58.5 us
    reduce_scatter x1, waiting for transfers between devices, on_device(): lax.psum_scatter(down.reshape(local * owners * capacity, model_width), 't...  58 us
    all_to_all x1, waiting for transfers between devices, on_device(): lax.all_to_all(back_send, 'expert', split_axis=0, concat_axis=0, tiled=True)  28.9 us
    all_to_all x1, starting transfers between devices, on_device(): lax.all_to_all(back_send, 'expert', split_axis=0, concat_axis=0, tiled=True)  13.8 us
    psum x1, blocking collectives, on_device(): owner_total = lax.psum(owner_part, 'dp')  8.4 us
    dot_general x1, matrix products, on_device(): jnp.einsum('erh,ehd->erd', hidden, w_down, preferred_element_type=jnp.flo...  8.22 us
  transfers between devices with their start and end apart: 3, of which 3 were waited for; matrix products, arithmetic and copies ran while one was open for 4% of the time, Pallas kernels for 0%

profile of v9, /device:TPU:1, one launch (start us, length us, event | category | flops | bytes accessed | tf_op | source)
XLA Modules:
  0.0 293.1 jit_solution(15573876256993716234)
XLA Ops:
  7.2 0.9 copy.59
  8.1 0.1 eq.71
  8.2 0.1 eq.75
  8.3 0.8 copy.64
  9.1 0.1 mul.46
  9.2 0.1 fusion.25
  9.3 0.1 convert_element_type.69
  9.5 1.2 reduce-window.6
  10.7 0.2 slice_reduce_fusion
  10.9 0.1 fusion.23
  11.1 0.1 reduce_sum.39
  11.2 0.1 copy.62
  11.2 0.7 multiply_add_fusion
  11.9 0.1 copy.63
  12.0 0.5 fusion.2
  12.5 2.0 convolution_convert_fusion.1
  14.5 2.2 reshape_reshape.3
  16.7 1.1 fusion.14
  17.8 59.3 %all_to_all.10 = bf16[32,76,128]{2,1,0:T(8,128)(2,1)S(1)} all-to-all(bf16[32,76,128]{2,1,0:T(8,128)(2,1)S(1)} %fusion.14), channel_id=1, replica_groups=mesh['dp'=4,'expert'=32,'tensor'=8] {'expert'}, dimensions={0} | all-to-all | bytes 1245184 | tf_op jit(solution)/shard_map/all_to_all | solution.py:34
  77.1 0.8 copy-done.1
  78.0 0.1 copy.77
  78.1 1.1 copy.67
  79.2 2.3 reshape.191
  81.5 0.0 reduce-scatter.2.cloned.1.call-start
  81.5 58.5 %all-gather.2.cloned.1.call-done = bf16[576,4096]{1,0:T(8,128)(2,1)} async-done(((bf16[576,512]{1,0:T(8,128)(2,1)}), bf16[576,4096]{1,0:T(8,128)(2,1)}) %all-gather.2.cloned.1.call-update) | async-done | bytes 4718608 | tf_op jit(solution)/shard_map/all_gather | solution.py:38
  140.0 5.5 %fusion.32 = f32[2,288,192]{2,1,0:T(8,128)} fusion(bf16[2,288,4096]{2,1,0:T(8,128)(2,1)} %bitcast.54, bf16[2,4096,192]{1,2,0:T(8,128)(2,1)} %param.13), kind=kOutput, calls=%fused_computation.48 | convolution fusion | flops 905969664 | bytes 8306688 | tf_op jit(solution)/shard_map/erd,edh->erh/dot_general | solution.py:41
  145.6 8.2 %convolution_convert_fusion = bf16[2,288,4096]{2,1,0:T(8,128)(2,1)} fusion(bf16[2,192,4096]{2,1,0:T(8,128)(2,1)S(1)} %copy-done, bf16[2,288,4096]{2,1,0:T(8,128)(2,1)} %bitcast.55, bf16[2,4096,192]{1,2,0:T(8,128)(2,1)} %param.14, f32[2,288,192]{2,1,0:T(8,128)} %fusion.32), kind=kOutput, calls=%fused_computation | convolution fusion | flops 1814962176 | bytes 16171008 | tf_op jit(solution)/shard_map/erh,ehd->erd/dot_general | solution.py:44
  153.8 0.9 fusion.29
  154.7 8.4 %psum.7 = bf16[2]{0:T(256)(128)(2,1)S(1)} all-reduce(f32[2]{0:T(128)S(1)} %fusion.29), channel_id=1, replica_groups=mesh['dp'=4,'expert'=32,'tensor'=8] {'dp'}, use_global_device_ids=true, to_apply=%region_7.8 | all-reduce | flops 2 | bytes 12 | tf_op jit(solution)/shard_map/psum | solution.py:53
  163.1 58.0 %reduce-scatter.2.cloned.1.call-done = bf16[576,512]{1,0:T(8,128)(2,1)} async-done(((bf16[576,4096]{1,0:T(8,128)(2,1)}), bf16[576,512]{1,0:T(8,128)(2,1)}) %reduce-scatter.2.cloned.1.call-update) | async-done | bytes 589840 | tf_op jit(solution)/shard_map/reduce_scatter | solution.py:47
  221.2 2.3 reshape.194
  223.4 1.2 copy.68
  224.6 0.2 copy.69
  224.9 0.9 pad_maximum_fusion
  225.8 13.8 %all-to-all-start.1 = ((bf16[32,76,128]{2,1,0:T(8,128)(2,1)}), bf16[32,76,128]{2,1,0:T(8,128)(2,1)}, u32[]{:S(2)}, u32[]{:S(2)}) async-start(bf16[32,76,128]{2,1,0:T(8,128)(2,1)} %pad_maximum_fusion), calls=%async_computation.2 | async-start | bytes 1310720 | tf_op jit(solution)/shard_map/all_to_all | solution.py:59
  239.6 0.1 broadcast_in_dim.54
  239.7 0.5 select_reduce_fusion
  240.2 0.9 copy.72
  241.0 1.0 broadcast_in_dim.58
  242.0 0.1 copy.73
  242.1 1.2 broadcast_in_dim.59
  243.2 2.9 copy.74
  246.1 3.7 %broadcast_select_fusion = f32[4,64,32,72]{3,1,2,0:T(8,128)} fusion(f32[64,32,72]{2,0,1:T(8,128)} %copy.74, pred[4,72]{1,0:T(4,128)(4,1)S(1)} %broadcast_in_dim.54), kind=kLoop, calls=%fused_computation.3 | loop fusion | flops 589824 | bytes 2949408 | tf_op jit(solution)/shard_map/jit(_where)/select_n | solution.py:68
  249.8 28.9 %all-to-all-done.1 = bf16[32,76,128]{2,1,0:T(8,128)(2,1)} async-done(((bf16[32,76,128]{2,1,0:T(8,128)(2,1)}), bf16[32,76,128]{2,1,0:T(8,128)(2,1)}, u32[]{:S(2)}, u32[]{:S(2)}) %all-to-all-start.1) | async-done | bytes 622624 | tf_op jit(solution)/shard_map/all_to_all | solution.py:59
  278.7 0.9 fusion.28
  279.6 0.6 mul.53
  280.2 5.4 %fusion.11 = bf16[4,8,8,128]{3,2,1,0:T(8,128)(2,1)S(1)} fusion(f32[4,64,32,72]{3,1,2,0:T(8,128)} %broadcast_select_fusion, bf16[32,76,128]{2,1,0:T(8,128)(2,1)} %all-to-all-done.1), kind=kOutput, calls=%fused_computation.15 | convolution fusion | flops 956334080 | bytes 3047424 | tf_op jit(solution)/shard_map/qtoj,ojl->tql/dot_general | solution.py:74
  285.6 0.6 copy.83
  (14 shorter events, 0.2 us)
Async XLA Ops:
  7.2 138.4 %copy-start = (bf16[2,192,4096]{2,1,0:T(8,128)(2,1)S(1)}, bf16[2,192,4096]{2,1,0:T(8,128)(2,1)}, u32[]{:S(2)}) copy-start(bf16[2,192,4096]{2,1,0:T(8,128)(2,1)} %param.15) | copy-start | bytes 9437188
  7.2 132.9 %all-gather.2.cloned.1.call-start = ((), (), s32[]{:S(2)}) async-start(), calls=%async_computation.3 | async-start | bytes 5308416 | tf_op jit(solution)/shard_map/all_gather | solution.py:38
  77.1 0.8 copy-start.1
  81.5 139.7 %reduce-scatter.2.cloned.1.call-start = ((), (), s32[]{:S(2)}) async-start(), calls=%async_computation.4 | async-start | bytes 5308416 | tf_op jit(solution)/shard_map/reduce_scatter | solution.py:47
  225.8 52.9 %all-to-all-start.1 = ((bf16[32,76,128]{2,1,0:T(8,128)(2,1)}), bf16[32,76,128]{2,1,0:T(8,128)(2,1)}, u32[]{:S(2)}, u32[]{:S(2)}) async-start(bf16[32,76,128]{2,1,0:T(8,128)(2,1)} %pad_maximum_fusion), calls=%async_computation.2 | async-start | bytes 1310720 | tf_op jit(solution)/shard_map/all_to_all | solution.py:59
Sparse Core Ops, SparseCore 0:
  81.6 58.3 all-gather.1
  154.0 67.1 reduce-scatter.1
